TPU v7x, 256 devices: a whole 4x4x8 slice. The times are simulated.
256 devices in a mesh: row: 2 (over core), col: 2 (over x_lo), rhs: 64 (over z, y, x_hi).
Axes of the slice: x: 4 (x_hi: 2, x_lo: 2; x = x_hi * 2 + x_lo), y: 4, z: 8, core: 2. Of those that a mesh axis runs over, the one named last changes fastest.
Arguments:
- front: bfloat16 [4096, 4096], P(('row', 'rhs'), 'col'), as said below
- anc_weight: bfloat16 [1024, 4096], P(('row', 'rhs'), 'col'), may hold values from -0.1875 to 0.1875
- solved: bfloat16 [2048, 8192], P(('row', 'col'), 'rhs'), may hold values from -6 to 6
- owners: int32 [8], replicated, may hold values from 0 to 3, as said below
- indices: int32 [8, 128], replicated, may hold values from 0 to 511
- counts: int32 [8], replicated, may hold values from 64 to 128, as said below
- rhs_side: bfloat16 [4096, 8192], P('row', 'rhs'), may hold values from -6 to 6
Outputs:
- solution: bfloat16 [4096, 8192], P('row', 'rhs')
Inputs may be any that keep to these rules, and one draw needn't show every extreme that they name: `front`: zero above the diagonal; diagonal entries 1 or more. The 4 tiles of each aligned block of 4 tiles have 4 different owners, numbered row index times 2 plus col index. `counts`: rows at or past a tile's count are padding.
All inputs are finite; a program needn't handle non-finite values.
Results may differ from a plain program's by a relative error of at most 0.0038.
Values may be sent and summed in bfloat16 or wider, within the bound.
No kernel may reach another device: no remote copies, remote signals or barrier semaphores. Data moves between devices by JAX's collectives and lax.ppermute only.
A program may use at most 128 MiB of HBM per device.

v0:
```python
import jax
import jax.numpy as jnp
from jax import lax
from jax.sharding import PartitionSpec as P


def from_root(x, axis, root):
    mine = lax.axis_index(axis) == root
    return lax.psum(jnp.where(mine, x, jnp.zeros_like(x)), axis)


def on_device(front, anc_weight, solved, owners, indices, counts, rhs_side):
    row_count = lax.axis_size("row")
    col_count = lax.axis_size("col")
    tiles_block = row_count * col_count
    row_index = lax.axis_index("row")
    col_index = lax.axis_index("col")
    tile_rows = indices.shape[1]
    columns = solved.shape[1]
    self_id = row_index * col_count + col_index
    owner_grid = owners.reshape(row_count, tiles_block)
    mine = (owner_grid == self_id).astype(jnp.int32)
    position = jnp.sum(mine * jnp.arange(tiles_block, dtype=jnp.int32)[None, :], axis=1)
    tile_ids = jnp.arange(row_count, dtype=jnp.int32) * tiles_block + position
    local_rows = indices[tile_ids]
    live_rows = jnp.arange(tile_rows, dtype=jnp.int32)[None, :] < counts[tile_ids][:, None]
    picked = solved[local_rows.reshape(-1)].reshape(row_count, tile_rows, columns)
    picked = jnp.where(live_rows[:, :, None], picked, jnp.zeros_like(picked))
    block_owners = lax.dynamic_slice_in_dim(owners, row_index * tiles_block, tiles_block)
    outgoing = jnp.broadcast_to(picked[:, None], (row_count, col_count, tile_rows, columns))
    outgoing = outgoing.reshape(row_count * col_count * tile_rows, columns)
    received = lax.all_to_all(outgoing, ("row", "col"), split_axis=0, concat_axis=0, tiled=True)
    slot_rows = received.reshape(tiles_block, tile_rows, columns)
    anc_values = slot_rows[block_owners].reshape(tiles_block * tile_rows, columns)
    front_tile = lax.all_gather(front, "rhs", axis=0, tiled=True)
    width = front_tile.shape[1]
    anc_total = lax.dot_general(
        lax.all_gather(anc_weight, "rhs", axis=0, tiled=True),
        anc_values,
        (((0,), (0,)), ((), ())),
        preferred_element_type=jnp.float32,
    )
    rhs_values = rhs_side.astype(jnp.float32)
    solution_rows = jnp.zeros((width, columns), jnp.bfloat16)
    for step_index in reversed(range(row_count)):
        current = solution_rows

        def no_product():
            return jnp.zeros((width, columns), jnp.float32)

        wanted = jnp.logical_and(col_index == step_index, row_index > step_index)

        def front_product():
            return lax.dot_general(
                front_tile, current, (((0,), (0,)), ((), ())), preferred_element_type=jnp.float32
            )

        front_term = lax.cond(wanted, front_product, no_product)
        rounded = lax.optimization_barrier((anc_total + front_term).astype(jnp.bfloat16))
        shares = lax.all_gather(rounded[None], "row", axis=0, tiled=True)
        summed = jnp.sum(shares.astype(jnp.float32), axis=0)
        reduced = rhs_values - summed

        def solve_block():
            return jax.scipy.linalg.solve_triangular(
                front_tile.astype(jnp.float32), reduced, trans=1, lower=True
            )

        on_diagonal = jnp.logical_and(row_index == step_index, col_index == step_index)
        fresh = lax.cond(on_diagonal, solve_block, no_product).astype(jnp.bfloat16)
        shared = from_root(fresh, "col", row_index)
        solution_rows = jnp.where(row_index == step_index, shared, solution_rows)
    return solution_rows


def solution(mesh):
    placed = (
        P(("row", "rhs"), "col"),
        P(("row", "rhs"), "col"),
        P(("row", "col"), "rhs"),
        P(),
        P(),
        P(),
        P("row", "rhs"),
    )
    return jax.shard_map(
        on_device, mesh=mesh, in_specs=placed, out_specs=P("row", "rhs"), check_vma=False
    )
```

profile of v0, /device:TPU:6, one launch (start us, length us, event | category | flops | bytes accessed | tf_op | source)
XLA Modules:
  0.0 987.7 jit_solution(2549492993331266399)
XLA Ops:
  6.5 0.0 copy-start
  6.5 0.0 all-gather.7.cloned.1.call-start
  6.5 0.7 all-gather.7.cloned.1.call-update
  7.3 0.0 all-gather.9.cloned.1.call-start
  7.3 0.7 all-gather.9.cloned.1.call-update
  8.0 0.7 broadcast_compare_fusion
  8.7 0.1 eq.34
  8.8 0.1 select_reduce_fusion
  8.9 1.2 gather_fusion.1
  10.2 1.3 gather_fusion
  11.5 0.9 gather_fusion.2
  12.3 0.1 iota_compare_fusion.2
  12.4 0.1 broadcast_select_fusion.4
  12.5 0.7 broadcast_in_dim.20
  13.2 4.1 all-to-all-start
  17.3 0.7 compare_select_fusion.1
  18.0 2.0 all-to-all-done
  20.1 0.6 gather_fusion.3
  20.7 141.6 %all-gather.7.cloned.1.call-done = bf16[2048,2048]{1,0:T(8,128)(2,1)} async-done(((bf16[32,2048]{1,0:T(8,128)(2,1)}), bf16[2048,2048]{1,0:T(8,128)(2,1)}) %all-gather.7.cloned.1.call-update) | async-done | bytes 8388624 | tf_op jit(solution)/shard_map/all_gather | solution.py:35
  162.2 0.1 conditional.4
  162.2 0.1 broadcast.102
  162.3 118.8 %all-gather.9.cloned.1.call-done = bf16[512,2048]{1,0:T(8,128)(2,1)} async-done(((bf16[8,2048]{1,0:T(8,128)(2,1)}), bf16[512,2048]{1,0:T(8,128)(2,1)}) %all-gather.9.cloned.1.call-update) | async-done | bytes 2097168 | tf_op jit(solution)/shard_map/all_gather | solution.py:38
  281.1 3.2 add_convert_fusion.1
  284.3 0.0 all-gather.11.cloned.1.call-update
  284.4 0.0 all-reduce.3.cloned.1.call-start
  284.4 0.1 convert_element_type.52
  284.5 12.7 %all-gather.11.cloned.1.call-done = bf16[4096,128]{0,1:T(8,128)(2,1)} async-done(((bf16[2048,128]{0,1:T(8,128)(2,1)}), bf16[4096,128]{0,1:T(8,128)(2,1)}) %all-gather.11.cloned.1.call-update) | async-done | bytes 1048592 | tf_op jit(solution)/shard_map/all_gather | solution.py:60
  297.2 1.4 convert_element_type.55
  298.7 5.8 conditional.5
  298.7 0.9 broadcast.104
  304.4 0.8 broadcast_select_fusion.2
  305.3 0.0 all-reduce.3.cloned.1.call-update
  305.3 0.0 all-gather.13.cloned.1.call-start
  305.4 320.7 %all-reduce.3.cloned.1.call-done = bf16[2048,128]{1,0:T(8,128)(2,1)} async-done(((bf16[2048,128]{1,0:T(8,128)(2,1)}), bf16[2048,128]{1,0:T(8,128)(2,1)}) %all-reduce.3.cloned.1.call-update) | async-done | bytes 524304 | tf_op jit(solution)/shard_map/psum | solution.py:9
  626.1 0.1 conditional.6
  626.1 0.1 broadcast.105.clone
  626.3 2.1 add_convert_fusion
  628.4 0.0 all-gather.13.cloned.1.call-update
  628.4 0.0 all-reduce.5.cloned.1.call-start
  628.5 21.0 %all-gather.13.cloned.1.call-done = bf16[4096,128]{0,1:T(8,128)(2,1)} async-done(((bf16[2048,128]{0,1:T(8,128)(2,1)}), bf16[4096,128]{0,1:T(8,128)(2,1)}) %all-gather.13.cloned.1.call-update) | async-done | bytes 1048592 | tf_op jit(solution)/shard_map/all_gather | solution.py:60
  649.5 1.4 convert_element_type.56
  650.9 2.0 conditional.7
  650.9 0.9 broadcast.106
  652.9 0.0 copy-start.1
  652.9 0.8 broadcast_select_fusion.1
  653.7 0.0 all-reduce.5.cloned.1.call-update
  653.8 324.9 %all-reduce.5.cloned.1.call-done = bf16[2048,128]{1,0:T(8,128)(2,1)} async-done(((bf16[2048,128]{1,0:T(8,128)(2,1)}), bf16[2048,128]{1,0:T(8,128)(2,1)}) %all-reduce.5.cloned.1.call-update) | async-done | bytes 524304 | tf_op jit(solution)/shard_map/psum | solution.py:9
  978.7 1.9 broadcast_select_fusion.3
  (11 shorter events, 0.1 us)
Async XLA Ops:
  6.5 4.9 copy-start
  6.5 277.9 %copy-start.4 = (bf16[2048,128]{1,0:T(8,128)(2,1)S(1)}, bf16[2048,128]{1,0:T(8,128)(2,1)}, u32[]{:S(2)}) copy-start(bf16[2048,128]{1,0:T(8,128)(2,1)} %param.23) | copy-start | bytes 1572868
  6.5 155.7 %all-gather.7.cloned.1.call-start = ((), (), s32[]{:S(2)}) async-start(), calls=%async_computation.1 | async-start | bytes 8519680 | tf_op jit(solution)/shard_map/all_gather | solution.py:35
  7.3 273.9 %all-gather.9.cloned.1.call-start = ((), (), s32[]{:S(2)}) async-start(), calls=%async_computation.2 | async-start | bytes 2129920 | tf_op jit(solution)/shard_map/all_gather | solution.py:38
  13.2 6.9 all-to-all-start
  17.3 279.9 %all-gather.11.cloned.1.call-start = ((), (), s32[]{:S(2)}) async-start(), calls=%async_computation.5 | async-start | bytes 1572864 | tf_op jit(solution)/shard_map/all_gather | solution.py:60
  284.4 341.7 %all-reduce.3.cloned.1.call-start = ((), (), s32[]{:S(2)}) async-start(), calls=%async_computation.3 | async-start | bytes 1048576 | tf_op jit(solution)/shard_map/psum | solution.py:9
  305.3 344.2 %all-gather.13.cloned.1.call-start = ((), (), s32[]{:S(2)}) async-start(), calls=%async_computation.6 | async-start | bytes 1572864 | tf_op jit(solution)/shard_map/all_gather | solution.py:60
  628.4 350.3 %all-reduce.5.cloned.1.call-start = ((), (), s32[]{:S(2)}) async-start(), calls=%async_computation.4 | async-start | bytes 1048576 | tf_op jit(solution)/shard_map/psum | solution.py:9
  652.9 327.7 %copy-start.1 = (bf16[512,128]{1,0:T(8,128)(2,1)S(1)}, bf16[512,128]{1,0:T(8,128)(2,1)}, u32[]{:S(2)}) copy-start(bf16[512,128]{1,0:T(8,128)(2,1)} %param.19) | copy-start | bytes 393220
Sparse Core Ops, SparseCore 0:
  10.8 151.3 all-gather.6
  165.8 115.2 all-gather.8
  284.5 12.6 all-gather.10
  305.4 320.6 all-reduce.2
  628.5 20.9 all-gather.12
  653.9 324.7 all-reduce.4
where the time goes:
time: 996 us; the launch traced here: 988 us
  waiting for transfers between devices  943 us (95%)
  between operations  13.9 us (1%)
  other arithmetic  10.4 us (1%)
    psum x2, waiting for transfers between devices, from_root(): return lax.psum(jnp.where(mine, x, jnp.zeros_like(x)), axis)  646 us
    all_gather x1, waiting for transfers between devices, on_device(): front_tile = lax.all_gather(front, 'rhs', axis=0, tiled=True)  142 us
    all_gather x1, waiting for transfers between devices, on_device(): lax.all_gather(anc_weight, 'rhs', axis=0, tiled=True)  119 us
    all_gather x2, waiting for transfers between devices, on_device(): shares = lax.all_gather(rounded[None], 'row', axis=0, tiled=True)  33.7 us
  transfers between devices with their start and end apart: 7, of which 7 were waited for; matrix products, arithmetic and copies ran while one was open for 1% of the time, Pallas kernels for 0%

commit v1 on v0

v1 whole, which is shorter than its diff:
```python
import jax
import jax.numpy as jnp
from jax import lax
from jax.sharding import PartitionSpec as P

BLOCK = 128
HIGH = lax.Precision.HIGHEST


def split_dot_t(mat_bf16, vec_f32):
    hi = vec_f32.astype(jnp.bfloat16)
    lo = (vec_f32 - hi.astype(jnp.float32)).astype(jnp.bfloat16)
    dims = (((0,), (0,)), ((), ()))
    out = lax.dot_general(mat_bf16, hi, dims, preferred_element_type=jnp.float32)
    return out + lax.dot_general(mat_bf16, lo, dims, preferred_element_type=jnp.float32)


def prepare(tile):
    n = tile.shape[0]
    nb = n // BLOCK
    blocks = jnp.stack(
        [tile[j * BLOCK:(j + 1) * BLOCK, j * BLOCK:(j + 1) * BLOCK] for j in range(nb)]
    ).astype(jnp.float32)
    eye = jnp.eye(BLOCK, dtype=jnp.float32)
    diag = jnp.sum(blocks * eye[None], axis=2)
    lower = jnp.tril(jnp.ones((BLOCK, BLOCK), jnp.bool_), -1)
    nil = jnp.where(lower[None], blocks / diag[:, :, None], 0.0)
    prod = eye[None] - nil
    power = nil
    steps = 1
    while 2 ** steps < BLOCK:
        power = jnp.einsum("bij,bjk->bik", power, power, precision=HIGH)
        prod = jnp.einsum("bij,bjk->bik", prod, eye[None] + power, precision=HIGH)
        steps += 1
    return prod, 1.0 / diag


def apply_solve(tile, prod, inv_diag, rhs):
    n = tile.shape[0]
    nb = n // BLOCK
    cols = rhs.shape[1]

    def body(i, carry):
        rest, out = carry
        j = nb - 1 - i
        r_j = lax.dynamic_slice_in_dim(rest, j * BLOCK, BLOCK, 0)
        p_j = lax.dynamic_index_in_dim(prod, j, 0, keepdims=False)
        d_j = lax.dynamic_index_in_dim(inv_diag, j, 0, keepdims=False)
        v_j = jnp.einsum("ji,jk->ik", p_j, r_j, precision=HIGH) * d_j[:, None]
        rows = lax.dynamic_slice_in_dim(tile, j * BLOCK, BLOCK, 0)
        rest = rest - split_dot_t(rows, v_j)
        out = lax.dynamic_update_slice_in_dim(out, v_j, j * BLOCK, 0)
        return rest, out

    _, out = lax.fori_loop(0, nb, body, (rhs, jnp.zeros((n, cols), jnp.float32)))
    return out


def on_device(front, anc_weight, solved, owners, indices, counts, rhs_side):
    row_count = lax.axis_size("row")
    col_count = lax.axis_size("col")
    tiles_block = row_count * col_count
    row_index = lax.axis_index("row")
    col_index = lax.axis_index("col")
    tile_rows = indices.shape[1]
    columns = solved.shape[1]
    self_id = row_index * col_count + col_index
    owner_grid = owners.reshape(row_count, tiles_block)
    mine = (owner_grid == self_id).astype(jnp.int32)
    position = jnp.sum(mine * jnp.arange(tiles_block, dtype=jnp.int32)[None, :], axis=1)
    tile_ids = jnp.arange(row_count, dtype=jnp.int32) * tiles_block + position
    local_rows = indices[tile_ids]
    live_rows = jnp.arange(tile_rows, dtype=jnp.int32)[None, :] < counts[tile_ids][:, None]
    picked = solved[local_rows.reshape(-1)].reshape(row_count, tile_rows, columns)
    picked = jnp.where(live_rows[:, :, None], picked, jnp.zeros_like(picked))
    block_owners = lax.dynamic_slice_in_dim(owners, row_index * tiles_block, tiles_block)
    outgoing = jnp.broadcast_to(picked[:, None], (row_count, col_count, tile_rows, columns))
    outgoing = outgoing.reshape(row_count * col_count * tile_rows, columns)
    received = lax.all_to_all(outgoing, ("row", "col"), split_axis=0, concat_axis=0, tiled=True)
    slot_rows = received.reshape(tiles_block, tile_rows, columns)
    anc_values = slot_rows[block_owners].reshape(tiles_block * tile_rows, columns)
    weight_tile = lax.all_gather(anc_weight, "rhs", axis=0, tiled=True)
    front_tile = lax.all_gather(front, "rhs", axis=0, tiled=True)
    width = front_tile.shape[1]
    anc_total = lax.dot_general(
        weight_tile, anc_values, (((0,), (0,)), ((), ())), preferred_element_type=jnp.float32
    )
    prod, inv_diag = prepare(front_tile)
    rhs_values = rhs_side.astype(jnp.float32)
    down = [(1, 0)]
    left = [(1, 0)]
    right = [(0, 1)]

    own_one = anc_total.astype(jnp.bfloat16)
    other_one = lax.ppermute(own_one, "row", [(0, 1)])
    reduced_one = rhs_values - own_one.astype(jnp.float32) - other_one.astype(jnp.float32)
    sol_one = apply_solve(front_tile, prod, inv_diag, reduced_one).astype(jnp.bfloat16)
    got_one = lax.ppermute(sol_one, "col", left)
    sol_one = jnp.where(col_index == 1, sol_one, got_one)

    own_zero = (anc_total + split_dot_t(front_tile, sol_one.astype(jnp.float32))).astype(jnp.bfloat16)
    own_zero = jnp.where(row_index == 0, anc_total.astype(jnp.bfloat16), own_zero)
    other_zero = lax.ppermute(own_zero, "row", down)
    reduced_zero = rhs_values - own_zero.astype(jnp.float32) - other_zero.astype(jnp.float32)
    sol_zero = apply_solve(front_tile, prod, inv_diag, reduced_zero).astype(jnp.bfloat16)
    got_zero = lax.ppermute(sol_zero, "col", right)
    sol_zero = jnp.where(col_index == 0, sol_zero, got_zero)
    return jnp.where(row_index == 1, sol_one, sol_zero)


def solution(mesh):
    placed = (
        P(("row", "rhs"), "col"),
        P(("row", "rhs"), "col"),
        P(("row", "col"), "rhs"),
        P(),
        P(),
        P(),
        P("row", "rhs"),
    )
    return jax.shard_map(
        on_device, mesh=mesh, in_specs=placed, out_specs=P("row", "rhs"), check_vma=False
    )
```

time: 996 us -> 493 us (0.49)
  waiting for transfers between devices: 943 us -> 282 us
  matrix products: 3.21 us -> 152 us
  local copies, waits for them, and re-layouts: 6.65 us -> 20.6 us
    psum x2 -> x0, waiting for transfers between devices: 646 us -> none  [from_root(): return lax.psum(jnp.where(mine, x, jnp.zeros_like(x)), axis)]
    dot_general x1 -> x111, matrix products: 3.21 us -> 152 us  [the longest x33 51.9 us: split_dot_t(): lax.dot_general(mat_bf16, lo, dims, preferred_element_type=jnp.float32)]
    all_gather x3 -> x1, waiting for transfers between devices: 153 us -> 110 us  [on_device(): weight_tile = lax.all_gather(anc_weight, 'rhs', axis=0, tiled=True)]
    ppermute x0 -> x4, waiting for transfers between devices: none -> 25.3 us  [the longest x1 14.7 us: on_device(): got_zero = lax.ppermute(sol_zero, 'col', right)]
    unnamed x6 -> x24, local copies, waits for them, and re-layouts: 0.01 us -> 12.7 us
  transfers between devices with their start and end apart: 7 -> 7, of which waited for: 7 -> 7; matrix products, arithmetic and copies ran while one was open for 1% -> 3% of each run, Pallas kernels for 0% -> 0%
where the time goes in v1:
time: 493 us; the launch traced here: 485 us
  waiting for transfers between devices  282 us (57%)
  matrix products  152 us (31%)
  local copies, waits for them, and re-layouts  20.6 us (4%)
  between operations  13.7 us (3%)
  starting transfers between devices  9.95 us (2%)
  other arithmetic  5.61 us (1%)
    all_gather x1, waiting for transfers between devices, on_device(): front_tile = lax.all_gather(front, 'rhs', axis=0, tiled=True)  143 us
    all_gather x1, waiting for transfers between devices, on_device(): weight_tile = lax.all_gather(anc_weight, 'rhs', axis=0, tiled=True)  110 us
    dot_general x33, matrix products, split_dot_t(): lax.dot_general(mat_bf16, lo, dims, preferred_element_type=jnp.float32)  51.9 us
    dot_general x33, matrix products, split_dot_t(): lax.dot_general(mat_bf16, hi, dims, preferred_element_type=jnp.float32)  45.5 us
    dot_general x32, matrix products, body(): v_j = jnp.einsum('ji,jk->ik', p_j, r_j, precision=HIGH) * d_j[:, None]  36.7 us
    ppermute x1, waiting for transfers between devices, on_device(): got_zero = lax.ppermute(sol_zero, 'col', right)  14.7 us
    unnamed x24, local copies, waits for them, and re-layouts  12.7 us
  transfers between devices with their start and end apart: 7, of which 7 were waited for; matrix products, arithmetic and copies ran while one was open for 3% of the time, Pallas kernels for 0%

profile of v1, /device:TPU:6, one launch (start us, length us, event | category | flops | bytes accessed | tf_op | source)
XLA Modules:
  0.0 484.9 jit_solution(5792975368108984710)
XLA Ops:
  13.2 4.1 all-to-all-start
  18.0 2.0 all-to-all-done
  20.7 110.2 %all-gather.3.cloned.1.call-done = bf16[512,2048]{1,0:T(8,128)(2,1)} async-done(((bf16[8,2048]{1,0:T(8,128)(2,1)}), bf16[512,2048]{1,0:T(8,128)(2,1)}) %all-gather.3.cloned.1.call-update) | async-done | bytes 2097168 | tf_op jit(solution)/shard_map/all_gather | solution.py:82
  130.9 2.1 fusion.80
  137.0 1.5 copy.12
  138.6 142.6 %all-gather.5.cloned.1.call-done = bf16[2048,2048]{1,0:T(8,128)(2,1)} async-done(((bf16[32,2048]{1,0:T(8,128)(2,1)}), bf16[2048,2048]{1,0:T(8,128)(2,1)}) %all-gather.5.cloned.1.call-update) | async-done | bytes 8388624 | tf_op jit(solution)/shard_map/all_gather | solution.py:83
  293.8 1.5 fusion.45
  307.4 2.2 fusion.85
  309.7 64.9 %while.34 = (s32[]{:T(128)}, f32[2048,128]{1,0:T(8,128)S(1)}, bf16[2048,128]{1,0:T(8,128)(2,1)S(1)}, bf16[2048,2048]{1,0:T(8,128)(2,1)}, f32[16,128,128]{2,1,0:T...) while((s32[]{:T(128)}, f32[2048,128]{1,0:T(8,128)S(1)}, ...), condition=%wide.region_3.4_spmd, body=%wide.region_2.3_spmd.sunk | while | flops 160006144 | bytes 5639389 | solution.py:55
  312.3 1.5 fusion.124
  316.3 1.5 fusion.124
  320.4 1.5 fusion.124
  324.5 1.5 fusion.124
  328.5 1.5 fusion.124
  332.6 1.5 fusion.124
  336.6 1.5 fusion.124
  340.7 1.5 fusion.124
  344.7 1.5 fusion.124
  348.8 1.5 fusion.124
  352.8 1.5 fusion.124
  356.9 1.5 fusion.124
  361.0 1.5 fusion.124
  365.0 1.5 fusion.124
  369.1 1.5 fusion.124
  373.1 1.5 fusion.124
  374.6 1.9 collective-permute-start.1
  376.5 8.0 %collective-permute-done.1 = bf16[2048,128]{1,0:T(8,128)(2,1)S(1)} collective-permute-done((bf16[2048,128]{1,0:T(8,128)(2,1)S(1)}, bf16[2048,128]{1,0:T(8,128)(2,1)S(1)}, u32[]{:S(2)}, u32[]{:S(2)}) %collective-permute-start.1) | collective-permute-done | bytes 524320 | tf_op jit(solution)/shard_map/ppermute | solution.py:98
  384.6 4.8 fusion.48
  392.1 2.5 collective-permute-done.2
  396.3 64.9 %while.35 = (s32[]{:T(128)}, f32[2048,128]{1,0:T(8,128)S(1)}, bf16[2048,128]{1,0:T(8,128)(2,1)S(1)}, bf16[2048,2048]{1,0:T(8,128)(2,1)}, f32[16,128,128]{2,1,0:T...) while((s32[]{:T(128)}, f32[2048,128]{1,0:T(8,128)S(1)}, ...), condition=%wide.region_5.6_spmd, body=%wide.region_4.5_spmd.sunk | while | flops 160006144 | bytes 5639389 | solution.py:55
  397.5 1.4 fusion.129
  398.8 1.5 fusion.130
  402.9 1.5 fusion.130
  407.0 1.5 fusion.130
  411.0 1.5 fusion.130
  415.1 1.5 fusion.130
  419.1 1.5 fusion.130
  423.2 1.5 fusion.130
  427.2 1.5 fusion.130
  431.3 1.5 fusion.130
  435.4 1.5 fusion.130
  439.4 1.5 fusion.130
  443.5 1.5 fusion.130
  447.5 1.5 fusion.130
  451.6 1.5 fusion.130
  455.7 1.5 fusion.130
  459.7 1.5 fusion.130
  462.5 14.7 %collective-permute-done.3 = bf16[2048,128]{1,0:T(8,128)(2,1)S(1)} collective-permute-done((bf16[2048,128]{1,0:T(8,128)(2,1)S(1)}, bf16[2048,128]{1,0:T(8,128)(2,1)S(1)}, u32[]{:S(2)}, u32[]{:S(2)}) %collective-permute-start.3) | collective-permute-done | bytes 524320 | tf_op jit(solution)/shard_map/ppermute | solution.py:106
  (168 shorter events, 123.0 us)
Async XLA Ops:
  6.5 4.9 %copy-start = (bf16[512,128]{1,0:T(8,128)(2,1)S(1)}, bf16[512,128]{1,0:T(8,128)(2,1)}, u32[]{:S(2)}) copy-start(bf16[512,128]{1,0:T(8,128)(2,1)} %param.13) | copy-start | bytes 393220
  6.5 124.3 %all-gather.3.cloned.1.call-start = ((), (), s32[]{:S(2)}) async-start(), calls=%async_computation.1 | async-start | bytes 2129920 | tf_op jit(solution)/shard_map/all_gather | solution.py:82
  7.3 273.9 %all-gather.5.cloned.1.call-start = ((), (), s32[]{:S(2)}) async-start(), calls=%async_computation.2 | async-start | bytes 8519680 | tf_op jit(solution)/shard_map/all_gather | solution.py:83
  13.2 6.9 %all-to-all-start = ((bf16[4,128,128]{2,1,0:T(8,128)(2,1)}), bf16[4,128,128]{2,1,0:T(8,128)(2,1)S(1)}, u32[]{:S(2)}, u32[]{:S(2)}) async-start(bf16[4,128,128]{2,1,0:T(8,128)(2,1)} %bitcast.9), calls=%async_computation | async-start | bytes 262144 | tf_op jit(solution)/shard_map/all_to_all | solution.py:79
  133.0 2.8 collective-permute-start
  374.6 9.9 %collective-permute-start.1 = (bf16[2048,128]{1,0:T(8,128)(2,1)S(1)}, bf16[2048,128]{1,0:T(8,128)(2,1)S(1)}, u32[]{:S(2)}, u32[]{:S(2)}) collective-permute-start(bf16[2048,128]{1,0:T(8,128)(2,1)S(1)} %get-tuple-element.313), channel_id=1, source_target_pairs={{64,0},{65,1},{66,2},{67,3},{68,4},{69,5},{70,6},{71,7},{72,8},{73... | collective-permute-start | bytes 1572872 | tf_op jit(solution)/shard_map/ppermute | solution.py:98
  376.5 12.9 %slice-start = ((s8[8388608]{0:T(1024)(128)(4,1)}), s8[4194304]{0:T(1024)(128)(4,1)S(1)}, s32[]{:S(2)}) async-start(s8[8388608]{0:T(1024)(128)(4,1)} %bitcast.128), calls=%async_computation.3 | async-start | bytes 8388608
  384.6 4.8 slice-start.1
  390.8 1.3 copy-start.1
  390.8 3.8 collective-permute-start.2
  461.2 16.0 %collective-permute-start.3 = (bf16[2048,128]{1,0:T(8,128)(2,1)S(1)}, bf16[2048,128]{1,0:T(8,128)(2,1)S(1)}, u32[]{:S(2)}, u32[]{:S(2)}) collective-permute-start(bf16[2048,128]{1,0:T(8,128)(2,1)S(1)} %get-tuple-element.314), channel_id=1, source_target_pairs={{0,64},{1,65},{2,66},{3,67},{4,68},{5,69},{6,70},{7,71},{8,72},{9,... | collective-permute-start | bytes 1572872 | tf_op jit(solution)/shard_map/ppermute | solution.py:106
Sparse Core Ops, SparseCore 0:
  10.9 119.9 all-gather.2
  134.4 146.7 all-gather.4

commit v2 on v1

--- a/solution.py
+++ b/solution.py
@@ -79,8 +79,13 @@
     received = lax.all_to_all(outgoing, ("row", "col"), split_axis=0, concat_axis=0, tiled=True)
     slot_rows = received.reshape(tiles_block, tile_rows, columns)
     anc_values = slot_rows[block_owners].reshape(tiles_block * tile_rows, columns)
-    weight_tile = lax.all_gather(anc_weight, "rhs", axis=0, tiled=True)
-    front_tile = lax.all_gather(front, "rhs", axis=0, tiled=True)
+    w_rows = anc_weight.shape[0]
+    both = jnp.concatenate([anc_weight, front], axis=0)
+    for axis in ("xh", "y", "z"):
+        both = lax.all_gather(both, axis, axis=0, tiled=True)
+    both = both.reshape(-1, w_rows + front.shape[0], both.shape[1])
+    weight_tile = both[:, :w_rows].reshape(-1, both.shape[2])
+    front_tile = both[:, w_rows:].reshape(-1, both.shape[2])
     width = front_tile.shape[1]
     anc_total = lax.dot_general(
         weight_tile, anc_values, (((0,), (0,)), ((), ())), preferred_element_type=jnp.float32
@@ -109,15 +114,21 @@
 
 
 def solution(mesh):
+    dims = dict(mesh.shape)
+    rhs_split = (dims["rhs"] // 8, 4, 2)
+    sub = jax.sharding.Mesh(
+        mesh.devices.reshape(dims["row"], dims["col"], *rhs_split), ("row", "col", "z", "y", "xh")
+    )
+    rhs = ("z", "y", "xh")
     placed = (
-        P(("row", "rhs"), "col"),
-        P(("row", "rhs"), "col"),
-        P(("row", "col"), "rhs"),
+        P(("row",) + rhs, "col"),
+        P(("row",) + rhs, "col"),
+        P(("row", "col"), rhs),
         P(),
         P(),
         P(),
-        P("row", "rhs"),
+        P("row", rhs),
     )
     return jax.shard_map(
-        on_device, mesh=mesh, in_specs=placed, out_specs=P("row", "rhs"), check_vma=False
+        on_device, mesh=sub, in_specs=placed, out_specs=P("row", rhs), check_vma=False
     )

time: 493 us -> 400 us (0.81)
  waiting for transfers between devices: 282 us -> 164 us
  matrix products: 152 us -> 164 us
  blocking collectives: 0 us -> 8.21 us
  local copies, waits for them, and re-layouts: 20.6 us -> 26.6 us
    all_gather x2, waiting for transfers between devices: 253 us -> 134 us  [on_device(): both = lax.all_gather(both, axis, axis=0, tiled=True)]
    dot_general x32, matrix products: 36.7 us -> 46.3 us  [body(): v_j = jnp.einsum('ji,jk->ik', p_j, r_j, precision=HIGH) * d_j[:, None]]
    slice x0 -> x1, local copies, waits for them, and re-layouts: none -> 8.38 us  [on_device(): front_tile = both[:, w_rows:].reshape(-1, both.shape[2])]
    all_gather x0 -> x1, blocking collectives: none -> 8.21 us  [on_device(): both = lax.all_gather(both, axis, axis=0, tiled=True)]
    unnamed x24 -> x21, local copies, waits for them, and re-layouts: 12.7 us -> 11.5 us
  transfers between devices with their start and end apart: 7 -> 7, of which waited for: 7 -> 6; matrix products, arithmetic and copies ran while one was open for 3% -> 5% of each run, Pallas kernels for 0% -> 0%
where the time goes in v2:
time: 400 us; the launch traced here: 394 us
  waiting for transfers between devices  164 us (41%)
  matrix products  164 us (41%)
  local copies, waits for them, and re-layouts  26.6 us (7%)
  between operations  13.7 us (3%)
  starting transfers between devices  11.6 us (3%)
  blocking collectives  8.21 us (2%)
  other arithmetic  5.42 us (1%)
    all_gather x2, waiting for transfers between devices, on_device(): both = lax.all_gather(both, axis, axis=0, tiled=True)  134 us
    dot_general x33, matrix products, split_dot_t(): lax.dot_general(mat_bf16, lo, dims, preferred_element_type=jnp.float32)  52.9 us
    dot_general x33, matrix products, split_dot_t(): lax.dot_general(mat_bf16, hi, dims, preferred_element_type=jnp.float32)  46.6 us
    dot_general x32, matrix products, body(): v_j = jnp.einsum('ji,jk->ik', p_j, r_j, precision=HIGH) * d_j[:, None]  46.3 us
    ppermute x1, waiting for transfers between devices, on_device(): got_zero = lax.ppermute(sol_zero, 'col', right)  14.6 us
    unnamed x21, local copies, waits for them, and re-layouts  11.5 us
    ppermute x1, waiting for transfers between devices, on_device(): got_one = lax.ppermute(sol_one, 'col', left)  10.7 us
    slice x1, local copies, waits for them, and re-layouts, on_device(): front_tile = both[:, w_rows:].reshape(-1, both.shape[2])  8.38 us
  transfers between devices with their start and end apart: 7, of which 6 were waited for; matrix products, arithmetic and copies ran while one was open for 5% of the time, Pallas kernels for 0%

profile of v2, /device:TPU:6, one launch (start us, length us, event | category | flops | bytes accessed | tf_op | source)
XLA Modules:
  0.0 394.2 jit_solution(9273000973371263965)
XLA Ops:
  7.5 8.2 %all_gather.9 = bf16[80,2048]{1,0:T(8,128)(2,1)} all-gather(bf16[40,2048]{1,0:T(8,128)(2,1)S(1)} %pad_maximum_fusion), channel_id=1, replica_groups=mesh['row'=2,'col'=2,'z'=8,'y'=4,'xh'=2] {'xh'}, dimensions={0}, use_global_device_ids=true | all-gather | bytes 491520 | tf_op jit(solution)/shard_map/all_gather | solution.py:85
  15.8 30.4 %all-gather.3.cloned.1.call-done = bf16[320,2048]{1,0:T(8,128)(2,1)} async-done(((bf16[80,2048]{1,0:T(8,128)(2,1)}), bf16[320,2048]{1,0:T(8,128)(2,1)}) %all-gather.3.cloned.1.call-update) | async-done | bytes 1310736 | tf_op jit(solution)/shard_map/all_gather | solution.py:85
  51.4 4.1 %all-to-all-start = ((bf16[4,128,128]{2,1,0:T(8,128)(2,1)}), bf16[4,128,128]{2,1,0:T(8,128)(2,1)S(1)}, u32[]{:S(2)}, u32[]{:S(2)}) async-start(bf16[4,128,128]{2,1,0:T(8,128)(2,1)} %bitcast.11), calls=%async_computation | async-start | bytes 262144 | tf_op jit(solution)/shard_map/all_to_all | solution.py:79
  56.3 1.9 all-to-all-done
  58.9 103.4 %all-gather.5.cloned.1.call-done = bf16[2560,2048]{1,0:T(8,128)(2,1)} async-done(((bf16[320,2048]{1,0:T(8,128)(2,1)}), bf16[2560,2048]{1,0:T(8,128)(2,1)}) %all-gather.5.cloned.1.call-update) | async-done | bytes 10485776 | tf_op jit(solution)/shard_map/all_gather | solution.py:85
  162.3 8.4 %slice.81 = bf16[64,32,2048]{2,1,0:T(8,128)(2,1)} slice(bf16[64,40,2048]{2,1,0:T(8,128)(2,1)} %bitcast.141), slice={[0:64], [8:40], [0:2048]} | slice | bytes 16777216 | tf_op jit(solution)/shard_map/slice | solution.py:88
  183.3 1.5 fusion.45
  187.3 2.3 fusion.80
  189.6 1.8 collective-permute-start
  200.8 2.2 fusion.85
  204.0 74.3 %while.34 = (s32[]{:T(128)}, f32[2048,128]{1,0:T(8,128)S(1)}, bf16[2048,128]{1,0:T(8,128)(2,1)}, bf16[2048,2048]{1,0:T(8,128)(2,1)}, f32[16,128,128]{2,1,0:T(8,1...) while((s32[]{:T(128)}, f32[2048,128]{1,0:T(8,128)S(1)}, ...), condition=%wide.region_3.4_spmd, body=%wide.region_2.3_spmd.sunk | while | flops 160006144 | bytes 5639397 | solution.py:55
  204.0 1.7 constant_dynamic-update-slice_fusion.4
  207.2 1.5 fusion.123
  208.7 1.8 constant_dynamic-update-slice_fusion.4
  211.8 1.5 fusion.123
  213.3 1.8 constant_dynamic-update-slice_fusion.4
  216.4 1.5 fusion.123
  218.0 1.8 constant_dynamic-update-slice_fusion.4
  221.1 1.5 fusion.123
  222.6 1.8 constant_dynamic-update-slice_fusion.4
  225.7 1.5 fusion.123
  227.3 1.8 constant_dynamic-update-slice_fusion.4
  230.4 1.5 fusion.123
  231.9 1.8 constant_dynamic-update-slice_fusion.4
  235.0 1.5 fusion.123
  236.6 1.8 constant_dynamic-update-slice_fusion.4
  241.2 1.8 constant_dynamic-update-slice_fusion.4
  244.3 1.5 fusion.123
  245.9 1.8 constant_dynamic-update-slice_fusion.4
  249.0 1.5 fusion.123
  250.5 1.8 constant_dynamic-update-slice_fusion.4
  255.2 1.8 constant_dynamic-update-slice_fusion.4
  258.3 1.5 fusion.123
  259.8 1.8 constant_dynamic-update-slice_fusion.4
  264.5 1.8 constant_dynamic-update-slice_fusion.4
  269.1 1.8 constant_dynamic-update-slice_fusion.4
  272.2 1.5 fusion.123
  273.8 1.8 constant_dynamic-update-slice_fusion.4
  278.4 3.0 collective-permute-start.1
  281.4 10.7 %collective-permute-done.1 = bf16[2048,128]{1,0:T(8,128)(2,1)S(1)} collective-permute-done((bf16[2048,128]{1,0:T(8,128)(2,1)}, bf16[2048,128]{1,0:T(8,128)(2,1)S(1)}, u32[]{:S(2)}, u32[]{:S(2)}) %collective-permute-start.1) | collective-permute-done | bytes 524320 | tf_op jit(solution)/shard_map/ppermute | solution.py:103
  293.2 5.8 %fusion.48 = f32[2048,128]{1,0:T(8,128)S(1)} fusion(bf16[2048,2048]{1,0:T(8,128)(2,1)} %get-tuple-element.503, bf16[2048,128]{1,0:T(8,128)(2,1)S(1)} %broadcast_select_fusion), kind=kOutput, calls=%fused_computation.68 | convolution fusion | flops 1074528256 | bytes 9961472 | tf_op jit(solution)/shard_map/dot_general | solution.py:15
  299.1 2.5 fusion.28
  302.9 2.5 collective-permute-done.2
  305.7 64.9 %while.35 = (s32[]{:T(128)}, f32[2048,128]{1,0:T(8,128)S(1)}, bf16[2048,128]{1,0:T(8,128)(2,1)S(1)}, bf16[2048,2048]{1,0:T(8,128)(2,1)}, f32[16,128,128]{2,1,0:T...) while((s32[]{:T(128)}, f32[2048,128]{1,0:T(8,128)S(1)}, ...), condition=%wide.region_5.6_spmd, body=%wide.region_4.5_spmd.sunk | while | flops 160006144 | bytes 5639397 | solution.py:55
  332.6 1.5 fusion.129
  344.8 1.5 fusion.129
  365.1 1.5 fusion.129
  371.9 14.6 %collective-permute-done.3 = bf16[2048,128]{1,0:T(8,128)(2,1)S(1)} collective-permute-done((bf16[2048,128]{1,0:T(8,128)(2,1)S(1)}, bf16[2048,128]{1,0:T(8,128)(2,1)S(1)}, u32[]{:S(2)}, u32[]{:S(2)}) %collective-permute-start.3) | collective-permute-done | bytes 524320 | tf_op jit(solution)/shard_map/ppermute | solution.py:111
  (164 shorter events, 127.1 us)
Async XLA Ops:
  6.5 43.1 %copy-start = (bf16[512,128]{1,0:T(8,128)(2,1)S(1)}, bf16[512,128]{1,0:T(8,128)(2,1)}, u32[]{:S(2)}) copy-start(bf16[512,128]{1,0:T(8,128)(2,1)} %param.13) | copy-start | bytes 393220
  6.5 39.6 %all-gather.3.cloned.1.call-start = ((), (), s32[]{:S(2)}) async-start(), calls=%async_computation.1 | async-start | bytes 1638400 | tf_op jit(solution)/shard_map/all_gather | solution.py:85
  15.7 146.5 %all-gather.5.cloned.1.call-start = ((), (), s32[]{:S(2)}) async-start(), calls=%async_computation.2 | async-start | bytes 11796480 | tf_op jit(solution)/shard_map/all_gather | solution.py:85
  51.4 6.9 %all-to-all-start = ((bf16[4,128,128]{2,1,0:T(8,128)(2,1)}), bf16[4,128,128]{2,1,0:T(8,128)(2,1)S(1)}, u32[]{:S(2)}, u32[]{:S(2)}) async-start(bf16[4,128,128]{2,1,0:T(8,128)(2,1)} %bitcast.11), calls=%async_computation | async-start | bytes 262144 | tf_op jit(solution)/shard_map/all_to_all | solution.py:79
  189.6 13.4 %collective-permute-start = (bf16[2048,128]{1,0:T(8,128)(2,1)S(1)}, bf16[2048,128]{1,0:T(8,128)(2,1)S(1)}, u32[]{:S(2)}, u32[]{:S(2)}) collective-permute-start(bf16[2048,128]{1,0:T(8,128)(2,1)S(1)} %get-tuple-element.343), channel_id=1, source_target_pairs={{0,128},{1,129},{2,130},{3,131},{4,132},{5,133},{6,134},{7,135},{8... | collective-permute-start | bytes 1572872 | tf_op jit(solution)/shard_map/ppermute | solution.py:100
  196.1 6.9 %copy-start.2 = (bf16[2048,128]{1,0:T(8,128)(2,1)S(1)}, bf16[2048,128]{1,0:T(8,128)(2,1)}, u32[]{:S(2)}) copy-start(bf16[2048,128]{1,0:T(8,128)(2,1)} %param.17) | copy-start | bytes 1572868
  278.4 13.8 %collective-permute-start.1 = (bf16[2048,128]{1,0:T(8,128)(2,1)}, bf16[2048,128]{1,0:T(8,128)(2,1)S(1)}, u32[]{:S(2)}, u32[]{:S(2)}) collective-permute-start(bf16[2048,128]{1,0:T(8,128)(2,1)} %get-tuple-element.313), channel_id=1, source_target_pairs={{64,0},{65,1},{66,2},{67,3},{68,4},{69,5},{70,6},{71,7},{72,8},{73... | collective-permute-start | bytes 1572872 | tf_op jit(solution)/shard_map/ppermute | solution.py:103
  281.4 17.7 %copy-start.1 = (bf16[2048,2048]{1,0:T(8,128)(2,1)S(1)}, bf16[2048,2048]{1,0:T(8,128)(2,1)}, u32[]{:S(2)}) copy-start(bf16[2048,2048]{1,0:T(8,128)(2,1)} %get-tuple-element.503) | copy-start | bytes 25165828
  301.6 3.8 collective-permute-start.2
  370.6 15.9 %collective-permute-start.3 = (bf16[2048,128]{1,0:T(8,128)(2,1)S(1)}, bf16[2048,128]{1,0:T(8,128)(2,1)S(1)}, u32[]{:S(2)}, u32[]{:S(2)}) collective-permute-start(bf16[2048,128]{1,0:T(8,128)(2,1)S(1)} %get-tuple-element.314), channel_id=1, source_target_pairs={{0,64},{1,65},{2,66},{3,67},{4,68},{5,69},{6,70},{7,71},{8,72},{9,... | collective-permute-start | bytes 1572872 | tf_op jit(solution)/shard_map/ppermute | solution.py:111
Sparse Core Ops, SparseCore 0:
  15.9 30.2 all-gather.2
  47.9 114.2 all-gather.4

commit v3 on v2

--- a/solution.py
+++ b/solution.py
@@ -2,6 +2,8 @@
 import jax.numpy as jnp
 from jax import lax
 from jax.sharding import PartitionSpec as P
+from jax.experimental import pallas as pl
+from jax.experimental.pallas import tpu as pltpu
 
 BLOCK = 128
 HIGH = lax.Precision.HIGHEST
@@ -33,6 +35,50 @@
         prod = jnp.einsum("bij,bjk->bik", prod, eye[None] + power, precision=HIGH)
         steps += 1
     return prod, 1.0 / diag
+
+
+def split_bf16(x):
+    hi = x.astype(jnp.bfloat16)
+    return hi, (x - hi.astype(jnp.float32)).astype(jnp.bfloat16)
+
+
+def solve_kernel(f_ref, p_ref, d_ref, r_ref, o_ref, rest_ref):
+    nb = p_ref.shape[0]
+    rest_ref[...] = r_ref[...]
+
+    def body(i, carry):
+        j = nb - 1 - i
+        start = pl.multiple_of(j * BLOCK, BLOCK)
+        r_hi, r_lo = split_bf16(rest_ref[:, pl.ds(start, BLOCK)])
+        p_hi, p_lo = split_bf16(p_ref[j])
+        v = jnp.dot(r_hi, p_hi, preferred_element_type=jnp.float32)
+        v = v + jnp.dot(r_lo, p_hi, preferred_element_type=jnp.float32)
+        v = v + jnp.dot(r_hi, p_lo, preferred_element_type=jnp.float32)
+        v = v * d_ref[pl.ds(j, 1), :]
+        v_hi, v_lo = split_bf16(v)
+        rows = f_ref[pl.ds(start, BLOCK), :]
+        upd = jnp.dot(v_hi, rows, preferred_element_type=jnp.float32)
+        upd = upd + jnp.dot(v_lo, rows, preferred_element_type=jnp.float32)
+        rest_ref[...] = rest_ref[...] - upd
+        o_ref[:, pl.ds(start, BLOCK)] = v.astype(o_ref.dtype)
+        return carry
+
+    lax.fori_loop(0, nb, body, 0)
+
+
+def kernel_solve(tile, prod, inv_diag, rhs):
+    n = tile.shape[0]
+    cols = rhs.shape[1]
+    vmem = pl.BlockSpec(memory_space=pltpu.VMEM)
+    out_t = pl.pallas_call(
+        solve_kernel,
+        out_shape=jax.ShapeDtypeStruct((cols, n), jnp.bfloat16),
+        in_specs=[vmem, vmem, vmem, vmem],
+        out_specs=vmem,
+        scratch_shapes=[pltpu.VMEM((cols, n), jnp.float32)],
+        compiler_params=pltpu.CompilerParams(vmem_limit_bytes=48 * 1024 * 1024),
+    )(tile, prod, inv_diag, rhs.T)
+    return out_t.T
 
 
 def apply_solve(tile, prod, inv_diag, rhs):
@@ -99,7 +145,7 @@
     own_one = anc_total.astype(jnp.bfloat16)
     other_one = lax.ppermute(own_one, "row", [(0, 1)])
     reduced_one = rhs_values - own_one.astype(jnp.float32) - other_one.astype(jnp.float32)
-    sol_one = apply_solve(front_tile, prod, inv_diag, reduced_one).astype(jnp.bfloat16)
+    sol_one = kernel_solve(front_tile, prod, inv_diag, reduced_one)
     got_one = lax.ppermute(sol_one, "col", left)
     sol_one = jnp.where(col_index == 1, sol_one, got_one)
 
@@ -107,7 +153,7 @@
     own_zero = jnp.where(row_index == 0, anc_total.astype(jnp.bfloat16), own_zero)
     other_zero = lax.ppermute(own_zero, "row", down)
     reduced_zero = rhs_values - own_zero.astype(jnp.float32) - other_zero.astype(jnp.float32)
-    sol_zero = apply_solve(front_tile, prod, inv_diag, reduced_zero).astype(jnp.bfloat16)
+    sol_zero = kernel_solve(front_tile, prod, inv_diag, reduced_zero)
     got_zero = lax.ppermute(sol_zero, "col", right)
     sol_zero = jnp.where(col_index == 0, sol_zero, got_zero)
     return jnp.where(row_index == 1, sol_one, sol_zero)

time: 400 us -> 280 us (0.70); the launches traced: 394 us -> 278 us
  matrix products: 164 us -> 23.9 us
  Pallas kernels: 0 us -> 26.4 us
    dot_general x33 -> x1, matrix products: 52.9 us -> 4.8 us  [split_dot_t(): lax.dot_general(mat_bf16, lo, dims, preferred_element_type=jnp.float32)]
    dot_general x32 -> x0, matrix products: 46.3 us -> none  [body(): v_j = jnp.einsum('ji,jk->ik', p_j, r_j, precision=HIGH) * d_j[:, None]]
    dot_general x33 -> x1, matrix products: 46.6 us -> 1.58 us  [split_dot_t(): lax.dot_general(mat_bf16, hi, dims, preferred_element_type=jnp.float32)]
    pallas_call x0 -> x2, Pallas kernels: none -> 26.4 us  [kernel_solve(): pl.pallas_call(solve_kernel, out_shape=jax.ShapeDtypeStruct((cols, n), jn...]
    unnamed x21 -> x24, local copies, waits for them, and re-layouts: 11.5 us -> 12.7 us
  transfers between devices with their start and end apart: 7 -> 7, of which waited for: 6 -> 6; matrix products, arithmetic and copies ran while one was open for 5% -> 7% of each run, Pallas kernels for 0% -> 0%
where the time goes in v3:
time: 280 us; the launch traced here: 278 us
  waiting for transfers between devices  163 us (58%)
  local copies, waits for them, and re-layouts  27.6 us (10%)
  Pallas kernels  26.4 us (9%)
  matrix products  23.9 us (9%)
  between operations  13.7 us (5%)
  starting transfers between devices  12.1 us (4%)
  blocking collectives  8.21 us (3%)
  other arithmetic  3.69 us (1%)
    all_gather x2, waiting for transfers between devices, on_device(): both = lax.all_gather(both, axis, axis=0, tiled=True)  134 us
    pallas_call x2, Pallas kernels, kernel_solve(): pl.pallas_call(solve_kernel, out_shape=jax.ShapeDtypeStruct((cols, n), jn...  26.4 us
    ppermute x1, waiting for transfers between devices, on_device(): got_zero = lax.ppermute(sol_zero, 'col', right)  15.9 us
    unnamed x24, local copies, waits for them, and re-layouts  12.7 us
    ppermute x1, waiting for transfers between devices, on_device(): got_one = lax.ppermute(sol_one, 'col', left)  9.89 us
    slice x1, local copies, waits for them, and re-layouts, on_device(): front_tile = both[:, w_rows:].reshape(-1, both.shape[2])  8.36 us
    all_gather x1, blocking collectives, on_device(): both = lax.all_gather(both, axis, axis=0, tiled=True)  8.21 us
    dot_general x6, matrix products, prepare(): prod = jnp.einsum('bij,bjk->bik', prod, eye[None] + power, precision=HIGH)  7.28 us
  transfers between devices with their start and end apart: 7, of which 6 were waited for; matrix products, arithmetic and copies ran while one was open for 7% of the time, Pallas kernels for 0%

profile of v3, /device:TPU:6, one launch (start us, length us, event | category | flops | bytes accessed | tf_op | source)
XLA Modules:
  0.0 278.4 jit_solution(2890403738194108825)
XLA Ops:
  6.5 1.0 pad_maximum_fusion
  7.5 8.2 %all_gather.9 = bf16[80,2048]{1,0:T(8,128)(2,1)} all-gather(bf16[40,2048]{1,0:T(8,128)(2,1)S(1)} %pad_maximum_fusion), channel_id=1, replica_groups=mesh['row'=2,'col'=2,'z'=8,'y'=4,'xh'=2] {'xh'}, dimensions={0}, use_global_device_ids=true | all-gather | bytes 491520 | tf_op jit(solution)/shard_map/all_gather | solution.py:131
  15.8 30.4 %all-gather.3.cloned.1.call-done = bf16[320,2048]{1,0:T(8,128)(2,1)} async-done(((bf16[80,2048]{1,0:T(8,128)(2,1)}), bf16[320,2048]{1,0:T(8,128)(2,1)}) %all-gather.3.cloned.1.call-update) | async-done | bytes 1310736 | tf_op jit(solution)/shard_map/all_gather | solution.py:131
  47.1 1.3 gather_fusion
  48.4 1.2 gather_fusion.1
  49.6 0.9 gather_fusion.2
  51.4 4.1 %all-to-all-start = ((bf16[4,128,128]{2,1,0:T(8,128)(2,1)}), bf16[4,128,128]{2,1,0:T(8,128)(2,1)S(1)}, u32[]{:S(2)}, u32[]{:S(2)}) async-start(bf16[4,128,128]{2,1,0:T(8,128)(2,1)} %bitcast.24), calls=%async_computation | async-start | bytes 262144 | tf_op jit(solution)/shard_map/all_to_all | solution.py:125
  55.5 1.2 copy.14
  58.9 103.4 %all-gather.5.cloned.1.call-done = bf16[2560,2048]{1,0:T(8,128)(2,1)} async-done(((bf16[320,2048]{1,0:T(8,128)(2,1)}), bf16[2560,2048]{1,0:T(8,128)(2,1)}) %all-gather.5.cloned.1.call-update) | async-done | bytes 10485776 | tf_op jit(solution)/shard_map/all_gather | solution.py:131
  162.3 8.4 %slice.80 = bf16[64,32,2048]{2,1,0:T(8,128)(2,1)} slice(bf16[64,40,2048]{2,1,0:T(8,128)(2,1)} %bitcast.134), slice={[0:64], [8:40], [0:2048]} | slice | bytes 16777216 | tf_op jit(solution)/shard_map/slice | solution.py:134
  171.4 0.8 fusion.51
  172.2 0.8 fusion.50
  172.9 0.8 fusion.49
  173.7 0.8 fusion.48
  174.5 0.8 fusion.47
  175.2 0.8 fusion.46
  176.0 0.8 fusion.45
  176.8 0.8 fusion.44
  177.5 0.8 fusion.43
  178.3 0.8 fusion.42
  179.1 0.8 fusion.41
  179.8 0.8 fusion.40
  180.6 0.8 fusion.39
  183.2 1.5 fusion.21
  184.7 1.4 fusion.18
  186.1 1.1 fusion.57
  187.3 3.1 %fusion.56 = (bf16[2048,128]{0,1:T(8,128)(2,1)S(1)}, f32[2048,128]{0,1:T(8,128)}) fusion(bf16[512,128]{1,0:T(8,128)(2,1)S(1)} %bitcast.136, bf16[64,40,2048]{2,1,0:T(8,128)(2,1)} %bitcast.135), kind=kOutput, calls=%fused_computation.100 | convolution fusion | flops 268697600 | bytes 3801088 | tf_op jit(solution)/shard_map/dot_general | solution.py:136
  190.3 1.8 collective-permute-start
  192.1 1.1 fusion.58
  193.3 1.2 fusion.16
  194.5 1.1 fusion.59
  195.6 1.2 fusion.14
  196.8 1.1 fusion.60
  197.9 1.2 fusion.12
  199.1 1.2 convolution_add_fusion.1
  200.3 1.2 fusion.10
  201.5 1.2 fusion.61.p_ref
  202.9 13.2 %shard_map.73 = bf16[128,2048]{1,0:T(8,128)(2,1)S(1)} custom-call(bf16[2048,2048]{1,0:T(8,128)(2,1)} %bitcast.128, f32[16,128,128]{2,1,0:T(8,128)S(1)} %fusion.61.p_ref, f32[16,128]{1,0:T(8,128)S(1)} %broadcast_divide_fusion.d_ref, f32[128,2048]{1,0:T(8,128)S(1)} %fusion.7.r_ref), custom_call_target="tpu_custom_call" | custom-call | tf_op jit(solution)/shard_map/pallas_call | solution.py:73
  216.1 3.6 %collective-permute-start.1 = (bf16[2048,128]{0,1:T(8,128)(2,1)S(1)}, bf16[2048,128]{0,1:T(8,128)(2,1)}, u32[]{:S(2)}, u32[]{:S(2)}) collective-permute-start(bf16[2048,128]{0,1:T(8,128)(2,1)S(1)} %bitcast.110), channel_id=1, source_target_pairs={{64,0},{65,1},{66,2},{67,3},{68,4},{69,5},{70,6},{71,7},{72,8},{73... | collective-permute-start | bytes 1572872 | tf_op jit(solution)/shard_map/ppermute | solution.py:149
  219.7 9.9 %collective-permute-done.1 = bf16[2048,128]{0,1:T(8,128)(2,1)} collective-permute-done((bf16[2048,128]{0,1:T(8,128)(2,1)S(1)}, bf16[2048,128]{0,1:T(8,128)(2,1)}, u32[]{:S(2)}, u32[]{:S(2)}) %collective-permute-start.1) | collective-permute-done | bytes 524320 | tf_op jit(solution)/shard_map/ppermute | solution.py:149
  229.7 4.8 %fusion.24 = f32[2048,128]{0,1:T(8,128)S(1)} fusion(bf16[2048,2048]{1,0:T(8,128)(2,1)} %bitcast.129, bf16[2048,128]{0,1:T(8,128)(2,1)S(1)} %broadcast_select_fusion), kind=kOutput, calls=%fused_computation.34 | convolution fusion | flops 1074528256 | bytes 9961472 | tf_op jit(solution)/shard_map/dot_general | solution.py:17
  234.5 1.6 fusion.2
  236.1 1.3 collective-permute-start.2
  237.4 2.5 collective-permute-done.2
  240.1 13.2 %shard_map.74 = bf16[128,2048]{1,0:T(8,128)(2,1)S(1)} custom-call(bf16[2048,2048]{1,0:T(8,128)(2,1)} %bitcast.130, f32[16,128,128]{2,1,0:T(8,128)S(1)} %fusion.61.p_ref, f32[16,128]{1,0:T(8,128)S(1)} %broadcast_divide_fusion.d_ref, f32[128,2048]{1,0:T(8,128)S(1)} %fusion.9.r_ref), custom_call_target="tpu_custom_call" | custom-call | tf_op jit(solution)/shard_map/pallas_call | solution.py:73
  253.3 1.3 collective-permute-start.3
  254.6 15.9 %collective-permute-done.3 = bf16[2048,128]{0,1:T(8,128)(2,1)S(1)} collective-permute-done((bf16[2048,128]{0,1:T(8,128)(2,1)S(1)}, bf16[2048,128]{0,1:T(8,128)(2,1)S(1)}, u32[]{:S(2)}, u32[]{:S(2)}) %collective-permute-start.3) | collective-permute-done | bytes 524320 | tf_op jit(solution)/shard_map/ppermute | solution.py:157
  270.6 1.0 copy.19
  (39 shorter events, 7.1 us)
Async XLA Ops:
  6.5 43.1 %copy-start = (bf16[512,128]{1,0:T(8,128)(2,1)S(1)}, bf16[512,128]{1,0:T(8,128)(2,1)}, u32[]{:S(2)}) copy-start(bf16[512,128]{1,0:T(8,128)(2,1)} %param.9) | copy-start | bytes 393220
  6.5 39.6 %all-gather.3.cloned.1.call-start = ((), (), s32[]{:S(2)}) async-start(), calls=%async_computation.1 | async-start | bytes 1638400 | tf_op jit(solution)/shard_map/all_gather | solution.py:131
  15.7 146.5 %all-gather.5.cloned.1.call-start = ((), (), s32[]{:S(2)}) async-start(), calls=%async_computation.2 | async-start | bytes 11796480 | tf_op jit(solution)/shard_map/all_gather | solution.py:131
  51.4 6.9 %all-to-all-start = ((bf16[4,128,128]{2,1,0:T(8,128)(2,1)}), bf16[4,128,128]{2,1,0:T(8,128)(2,1)S(1)}, u32[]{:S(2)}, u32[]{:S(2)}) async-start(bf16[4,128,128]{2,1,0:T(8,128)(2,1)} %bitcast.24), calls=%async_computation | async-start | bytes 262144 | tf_op jit(solution)/shard_map/all_to_all | solution.py:125
  190.3 12.4 %collective-permute-start = (bf16[2048,128]{0,1:T(8,128)(2,1)S(1)}, bf16[2048,128]{0,1:T(8,128)(2,1)S(1)}, u32[]{:S(2)}, u32[]{:S(2)}) collective-permute-start(bf16[2048,128]{0,1:T(8,128)(2,1)S(1)} %get-tuple-element.5), channel_id=1, source_target_pairs={{0,128},{1,129},{2,130},{3,131},{4,132},{5,133},{6,134},{7,135},{8... | collective-permute-start | bytes 1572872 | tf_op jit(solution)/shard_map/ppermute | solution.py:146
  216.1 13.4 %collective-permute-start.1 = (bf16[2048,128]{0,1:T(8,128)(2,1)S(1)}, bf16[2048,128]{0,1:T(8,128)(2,1)}, u32[]{:S(2)}, u32[]{:S(2)}) collective-permute-start(bf16[2048,128]{0,1:T(8,128)(2,1)S(1)} %bitcast.110), channel_id=1, source_target_pairs={{64,0},{65,1},{66,2},{67,3},{68,4},{69,5},{70,6},{71,7},{72,8},{73... | collective-permute-start | bytes 1572872 | tf_op jit(solution)/shard_map/ppermute | solution.py:149
  219.7 14.8 %slice-start = ((s8[8388608]{0:T(1024)(128)(4,1)}), s8[4194304]{0:T(1024)(128)(4,1)S(1)}, s32[]{:S(2)}) async-start(s8[8388608]{0:T(1024)(128)(4,1)} %bitcast.131), calls=%async_computation.3 | async-start | bytes 8388608
  219.7 14.8 %copy-start.1 = (f32[2048,128]{0,1:T(8,128)S(1)}, f32[2048,128]{0,1:T(8,128)}, u32[]{:S(2)}) copy-start(f32[2048,128]{0,1:T(8,128)} %get-tuple-element.6) | copy-start | bytes 3145732
  229.7 4.8 %slice-start.1 = ((s8[8388608]{0:T(1024)(128)(4,1)}), s8[4194304]{0:T(1024)(128)(4,1)S(1)}, s32[]{:S(2)}) async-start(s8[8388608]{0:T(1024)(128)(4,1)} %bitcast.131), calls=%async_computation.4 | async-start | bytes 8388608
  236.1 3.8 %collective-permute-start.2 = (bf16[2048,128]{0,1:T(8,128)(2,1)S(1)}, bf16[2048,128]{0,1:T(8,128)(2,1)S(1)}, u32[]{:S(2)}, u32[]{:S(2)}) collective-permute-start(bf16[2048,128]{0,1:T(8,128)(2,1)S(1)} %fusion.2), channel_id=1, source_target_pairs={{128,0},{129,1},{130,2},{131,3},{132,4},{133,5},{134,6},{135,7},{1... | collective-permute-start | bytes 1572872 | tf_op jit(solution)/shard_map/ppermute | solution.py:154
  253.3 17.2 %collective-permute-start.3 = (bf16[2048,128]{0,1:T(8,128)(2,1)S(1)}, bf16[2048,128]{0,1:T(8,128)(2,1)S(1)}, u32[]{:S(2)}, u32[]{:S(2)}) collective-permute-start(bf16[2048,128]{0,1:T(8,128)(2,1)S(1)} %bitcast.111), channel_id=1, source_target_pairs={{0,64},{1,65},{2,66},{3,67},{4,68},{5,69},{6,70},{7,71},{8,72},{9,... | collective-permute-start | bytes 1572872 | tf_op jit(solution)/shard_map/ppermute | solution.py:157
Sparse Core Ops, SparseCore 0:
  15.9 30.2 all-gather.2
  47.9 114.2 all-gather.4

commit v4 on v3

--- a/solution.py
+++ b/solution.py
@@ -17,12 +17,26 @@
     return out + lax.dot_general(mat_bf16, lo, dims, preferred_element_type=jnp.float32)
 
 
+def split_bf16(x):
+    hi = x.astype(jnp.bfloat16)
+    return hi, (x - hi.astype(jnp.float32)).astype(jnp.bfloat16)
+
+
+def mm3(a, b):
+    a_hi, a_lo = split_bf16(a)
+    b_hi, b_lo = split_bf16(b)
+    eq = "bij,bjk->bik"
+    out = jnp.einsum(eq, a_hi, b_hi, preferred_element_type=jnp.float32)
+    out = out + jnp.einsum(eq, a_lo, b_hi, preferred_element_type=jnp.float32)
+    return out + jnp.einsum(eq, a_hi, b_lo, preferred_element_type=jnp.float32)
+
+
 def prepare(tile):
     n = tile.shape[0]
     nb = n // BLOCK
-    blocks = jnp.stack(
-        [tile[j * BLOCK:(j + 1) * BLOCK, j * BLOCK:(j + 1) * BLOCK] for j in range(nb)]
-    ).astype(jnp.float32)
+    starts = jnp.arange(nb, dtype=jnp.int32) * BLOCK
+    blocks = jax.vmap(lambda s: lax.dynamic_slice(tile, (s, s), (BLOCK, BLOCK)))(starts)
+    blocks = blocks.astype(jnp.float32)
     eye = jnp.eye(BLOCK, dtype=jnp.float32)
     diag = jnp.sum(blocks * eye[None], axis=2)
     lower = jnp.tril(jnp.ones((BLOCK, BLOCK), jnp.bool_), -1)
@@ -31,15 +45,10 @@
     power = nil
     steps = 1
     while 2 ** steps < BLOCK:
-        power = jnp.einsum("bij,bjk->bik", power, power, precision=HIGH)
-        prod = jnp.einsum("bij,bjk->bik", prod, eye[None] + power, precision=HIGH)
+        power = mm3(power, power)
+        prod = mm3(prod, eye[None] + power)
         steps += 1
     return prod, 1.0 / diag
-
-
-def split_bf16(x):
-    hi = x.astype(jnp.bfloat16)
-    return hi, (x - hi.astype(jnp.float32)).astype(jnp.bfloat16)
 
 
 def solve_kernel(f_ref, p_ref, d_ref, r_ref, o_ref, rest_ref):

time: 280 us -> 308 us (1.10)
  local copies, waits for them, and re-layouts: 27.6 us -> 63.7 us
  Pallas kernels: 26.4 us -> 19.7 us
    gather x0 -> x48, local copies, waits for them, and re-layouts: none -> 46.1 us
    unnamed x24 -> x15, local copies, waits for them, and re-layouts: 12.7 us -> 3.42 us
    pallas_call x2, Pallas kernels: 26.4 us -> 19.7 us  [kernel_solve(): pl.pallas_call(solve_kernel, out_shape=jax.ShapeDtypeStruct((cols, n), jn...]
    dot_general x12 -> x36, matrix products: 14.5 us -> 13 us  [the longest x12 4.39 us: mm3(): return out + jnp.einsum(eq, a_hi, b_lo, preferred_element_type=jnp.float32)]
  transfers between devices with their start and end apart: 7 -> 7, of which waited for: 6 -> 6; matrix products, arithmetic and copies ran while one was open for 7% -> 6% of each run, Pallas kernels for 0% -> 0%
where the time goes in v4:
time: 308 us; the launch traced here: 306 us
  waiting for transfers between devices  163 us (53%)
  local copies, waits for them, and re-layouts  63.7 us (21%)
  matrix products  22.3 us (7%)
  Pallas kernels  19.7 us (6%)
  between operations  13.9 us (5%)
  starting transfers between devices  12.1 us (4%)
  blocking collectives  8.21 us (3%)
  other arithmetic  3.71 us (1%)
    all_gather x2, waiting for transfers between devices, on_device(): both = lax.all_gather(both, axis, axis=0, tiled=True)  134 us
    gather x48, local copies, waits for them, and re-layouts  46.1 us
    pallas_call x2, Pallas kernels, kernel_solve(): pl.pallas_call(solve_kernel, out_shape=jax.ShapeDtypeStruct((cols, n), jn...  19.7 us
    ppermute x1, waiting for transfers between devices, on_device(): got_zero = lax.ppermute(sol_zero, 'col', right)  15.9 us
    ppermute x1, waiting for transfers between devices, on_device(): got_one = lax.ppermute(sol_one, 'col', left)  9.88 us
    slice x1, local copies, waits for them, and re-layouts, on_device(): front_tile = both[:, w_rows:].reshape(-1, both.shape[2])  8.38 us
    all_gather x1, blocking collectives, on_device(): both = lax.all_gather(both, axis, axis=0, tiled=True)  8.21 us
  transfers between devices with their start and end apart: 7, of which 6 were waited for; matrix products, arithmetic and copies ran while one was open for 6% of the time, Pallas kernels for 0%

profile of v4, /device:TPU:6, one launch (start us, length us, event | category | flops | bytes accessed | tf_op | source)
XLA Modules:
  0.0 306.5 jit_solution(2382728909276438853)
XLA Ops:
  6.5 1.0 pad_maximum_fusion
  7.5 8.2 %all_gather.9 = bf16[80,2048]{1,0:T(8,128)(2,1)} all-gather(bf16[40,2048]{1,0:T(8,128)(2,1)S(1)} %pad_maximum_fusion), channel_id=1, replica_groups=mesh['row'=2,'col'=2,'z'=8,'y'=4,'xh'=2] {'xh'}, dimensions={0}, use_global_device_ids=true | all-gather | bytes 491520 | tf_op jit(solution)/shard_map/all_gather | solution.py:140
  15.8 30.4 %all-gather.3.cloned.1.call-done = bf16[320,2048]{1,0:T(8,128)(2,1)} async-done(((bf16[80,2048]{1,0:T(8,128)(2,1)}), bf16[320,2048]{1,0:T(8,128)(2,1)}) %all-gather.3.cloned.1.call-update) | async-done | bytes 1310736 | tf_op jit(solution)/shard_map/all_gather | solution.py:140
  46.2 0.7 broadcast_compare_fusion
  47.1 1.3 gather_fusion
  48.4 1.2 gather_fusion.1
  49.6 0.9 gather_fusion.2
  50.7 0.7 broadcast_in_dim.28
  51.4 4.1 %all-to-all-start = ((bf16[4,128,128]{2,1,0:T(8,128)(2,1)}), bf16[4,128,128]{2,1,0:T(8,128)(2,1)S(1)}, u32[]{:S(2)}, u32[]{:S(2)}) async-start(bf16[4,128,128]{2,1,0:T(8,128)(2,1)} %bitcast.8), calls=%async_computation | async-start | bytes 262144 | tf_op jit(solution)/shard_map/all_to_all | solution.py:134
  55.5 1.2 copy.14
  56.8 0.7 compare_select_fusion.1
  58.9 103.4 %all-gather.5.cloned.1.call-done = bf16[2560,2048]{1,0:T(8,128)(2,1)} async-done(((bf16[320,2048]{1,0:T(8,128)(2,1)}), bf16[2560,2048]{1,0:T(8,128)(2,1)}) %all-gather.5.cloned.1.call-update) | async-done | bytes 10485776 | tf_op jit(solution)/shard_map/all_gather | solution.py:140
  162.3 8.4 %slice.27 = bf16[64,32,2048]{2,1,0:T(8,128)(2,1)} slice(bf16[64,40,2048]{2,1,0:T(8,128)(2,1)} %bitcast.47), slice={[0:64], [8:40], [0:2048]} | slice | bytes 16777216 | tf_op jit(solution)/shard_map/slice | solution.py:143
  170.7 46.4 %while.1 = (s32[]{:T(128)}, bf16[2048,2048]{1,0:T(8,128)(2,1)}, s32[16,2]{0,1:T(2,128)S(1)}, bf16[16,128,128]{2,1,0:T(8,128)(2,1)S(1)}, s32[]{:T(128)}) while((s32[]{:T(128)}, bf16[2048,2048]{1,0:T(8,128)(2,1)}, s32[16,2]{0,1:T(2,128)S(1)}, bf16[16,128,128]{2,1,0:T(8,128)(2,1)S(1)}, s32[]{:T(128)}) %tuple.28), condition=%wide.while_cond, body=%wide.while_body.sunk | while | flops 2 | bytes 65653 | solution.py:38
  171.3 2.3 bitcast_dynamic-update-slice_fusion.2
  174.2 2.3 bitcast_dynamic-update-slice_fusion.2
  177.1 2.3 bitcast_dynamic-update-slice_fusion.2
  180.0 2.3 bitcast_dynamic-update-slice_fusion.2
  182.9 2.3 bitcast_dynamic-update-slice_fusion.2
  185.8 2.3 bitcast_dynamic-update-slice_fusion.2
  188.7 2.3 bitcast_dynamic-update-slice_fusion.2
  191.6 2.3 bitcast_dynamic-update-slice_fusion.2
  194.5 2.3 bitcast_dynamic-update-slice_fusion.2
  197.4 2.3 bitcast_dynamic-update-slice_fusion.2
  200.4 2.3 bitcast_dynamic-update-slice_fusion.2
  203.3 2.3 bitcast_dynamic-update-slice_fusion.2
  206.2 2.3 bitcast_dynamic-update-slice_fusion.2
  209.1 2.3 bitcast_dynamic-update-slice_fusion.2
  212.0 2.3 bitcast_dynamic-update-slice_fusion.2
  214.9 2.1 bitcast_dynamic-update-slice_fusion.2
  217.4 0.8 fusion.20
  218.2 0.9 convolution_add_fusion.24
  219.1 0.9 convolution_add_fusion.23
  220.7 3.1 fusion.75
  223.8 1.8 collective-permute-start
  235.7 0.7 slice-done
  236.4 1.4 slice-done.1
  237.9 9.9 %shard_map.73 = bf16[128,2048]{1,0:T(8,128)(2,1)S(1)} custom-call(bf16[2048,2048]{1,0:T(8,128)(2,1)S(1)} %bitcast.44, f32[16,128,128]{2,1,0:T(8,128)S(1)} %convolution_add_fusion.1.p_ref, f32[16,128]{1,0:T(8,128)S(1)} %broadcast_divide_fusion.d_ref, f32[128,2048]{1,0:T(8,128)S(1)} %fusion.8.r_ref), custom_call_target="tpu_custom_call" | custom-call | tf_op jit(solution)/shard_map/pallas_call | solution.py:82
  247.7 3.6 %collective-permute-start.1 = (bf16[2048,128]{0,1:T(8,128)(2,1)S(1)}, bf16[2048,128]{0,1:T(8,128)(2,1)}, u32[]{:S(2)}, u32[]{:S(2)}) collective-permute-start(bf16[2048,128]{0,1:T(8,128)(2,1)S(1)} %bitcast.40), channel_id=1, source_target_pairs={{64,0},{65,1},{66,2},{67,3},{68,4},{69,5},{70,6},{71,7},{72,8},{73... | collective-permute-start | bytes 1572872 | tf_op jit(solution)/shard_map/ppermute | solution.py:158
  251.3 9.9 %collective-permute-done.1 = bf16[2048,128]{0,1:T(8,128)(2,1)} collective-permute-done((bf16[2048,128]{0,1:T(8,128)(2,1)S(1)}, bf16[2048,128]{0,1:T(8,128)(2,1)}, u32[]{:S(2)}, u32[]{:S(2)}) %collective-permute-start.1) | collective-permute-done | bytes 524320 | tf_op jit(solution)/shard_map/ppermute | solution.py:158
  261.3 4.8 %fusion.11 = f32[2048,128]{0,1:T(8,128)S(1)} fusion(bf16[2048,2048]{1,0:T(8,128)(2,1)} %get-tuple-element.75, bf16[2048,128]{0,1:T(8,128)(2,1)S(1)} %broadcast_select_fusion), kind=kOutput, calls=%fused_computation.72 | convolution fusion | flops 1074528256 | bytes 9961472 | tf_op jit(solution)/shard_map/dot_general | solution.py:17
  266.1 1.4 fusion.2
  267.6 1.3 collective-permute-start.2
  268.9 2.5 collective-permute-done.2
  271.6 9.8 %shard_map.74 = bf16[128,2048]{1,0:T(8,128)(2,1)S(1)} custom-call(bf16[2048,2048]{1,0:T(8,128)(2,1)S(1)} %bitcast.46, f32[16,128,128]{2,1,0:T(8,128)S(1)} %convolution_add_fusion.1.p_ref, f32[16,128]{1,0:T(8,128)S(1)} %broadcast_divide_fusion.d_ref, f32[128,2048]{1,0:T(8,128)S(1)} %fusion.10.r_ref), custom_call_target="tpu_custom_call" | custom-call | tf_op jit(solution)/shard_map/pallas_call | solution.py:82
  281.4 1.3 collective-permute-start.3
  282.7 15.9 %collective-permute-done.3 = bf16[2048,128]{0,1:T(8,128)(2,1)S(1)} collective-permute-done((bf16[2048,128]{0,1:T(8,128)(2,1)S(1)}, bf16[2048,128]{0,1:T(8,128)(2,1)S(1)}, u32[]{:S(2)}, u32[]{:S(2)}) %collective-permute-start.3) | collective-permute-done | bytes 524320 | tf_op jit(solution)/shard_map/ppermute | solution.py:166
  298.6 1.0 copy.19
  (106 shorter events, 23.2 us)
Async XLA Ops:
  6.5 43.1 %copy-start = (bf16[512,128]{1,0:T(8,128)(2,1)S(1)}, bf16[512,128]{1,0:T(8,128)(2,1)}, u32[]{:S(2)}) copy-start(bf16[512,128]{1,0:T(8,128)(2,1)} %param.9) | copy-start | bytes 393220
  6.5 39.6 %all-gather.3.cloned.1.call-start = ((), (), s32[]{:S(2)}) async-start(), calls=%async_computation.1 | async-start | bytes 1638400 | tf_op jit(solution)/shard_map/all_gather | solution.py:140
  15.7 146.5 %all-gather.5.cloned.1.call-start = ((), (), s32[]{:S(2)}) async-start(), calls=%async_computation.2 | async-start | bytes 11796480 | tf_op jit(solution)/shard_map/all_gather | solution.py:140
  51.4 6.9 %all-to-all-start = ((bf16[4,128,128]{2,1,0:T(8,128)(2,1)}), bf16[4,128,128]{2,1,0:T(8,128)(2,1)S(1)}, u32[]{:S(2)}, u32[]{:S(2)}) async-start(bf16[4,128,128]{2,1,0:T(8,128)(2,1)} %bitcast.8), calls=%async_computation | async-start | bytes 262144 | tf_op jit(solution)/shard_map/all_to_all | solution.py:134
  223.8 11.7 %collective-permute-start = (bf16[2048,128]{0,1:T(8,128)(2,1)S(1)}, bf16[2048,128]{0,1:T(8,128)(2,1)S(1)}, u32[]{:S(2)}, u32[]{:S(2)}) collective-permute-start(bf16[2048,128]{0,1:T(8,128)(2,1)S(1)} %get-tuple-element.23), channel_id=1, source_target_pairs={{0,128},{1,129},{2,130},{3,131},{4,132},{5,133},{6,134},{7,135},{8... | collective-permute-start | bytes 1572872 | tf_op jit(solution)/shard_map/ppermute | solution.py:155
  234.2 2.2 slice-start
  234.9 3.0 slice-start.1
  247.7 13.4 %collective-permute-start.1 = (bf16[2048,128]{0,1:T(8,128)(2,1)S(1)}, bf16[2048,128]{0,1:T(8,128)(2,1)}, u32[]{:S(2)}, u32[]{:S(2)}) collective-permute-start(bf16[2048,128]{0,1:T(8,128)(2,1)S(1)} %bitcast.40), channel_id=1, source_target_pairs={{64,0},{65,1},{66,2},{67,3},{68,4},{69,5},{70,6},{71,7},{72,8},{73... | collective-permute-start | bytes 1572872 | tf_op jit(solution)/shard_map/ppermute | solution.py:158
  251.3 14.8 %slice-start.2 = ((s8[8388608]{0:T(1024)(128)(4,1)}), s8[4194304]{0:T(1024)(128)(4,1)S(1)}, s32[]{:S(2)}) async-start(s8[8388608]{0:T(1024)(128)(4,1)} %bitcast.45), calls=%async_computation.5 | async-start | bytes 8388608
  251.3 14.8 %copy-start.2 = (f32[2048,128]{0,1:T(8,128)S(1)}, f32[2048,128]{0,1:T(8,128)}, u32[]{:S(2)}) copy-start(f32[2048,128]{0,1:T(8,128)} %get-tuple-element.24) | copy-start | bytes 3145732
  261.2 4.8 %slice-start.3 = ((s8[8388608]{0:T(1024)(128)(4,1)}), s8[4194304]{0:T(1024)(128)(4,1)S(1)}, s32[]{:S(2)}) async-start(s8[8388608]{0:T(1024)(128)(4,1)} %bitcast.45), calls=%async_computation.6 | async-start | bytes 8388608
  266.1 33.5 %copy-start.1 = (bf16[512,128]{1,0:T(8,128)(2,1)S(1)}, bf16[512,128]{1,0:T(8,128)(2,1)}, u32[]{:S(2)}) copy-start(bf16[512,128]{1,0:T(8,128)(2,1)} %param.9) | copy-start | bytes 393220
  267.6 3.8 %collective-permute-start.2 = (bf16[2048,128]{0,1:T(8,128)(2,1)S(1)}, bf16[2048,128]{0,1:T(8,128)(2,1)S(1)}, u32[]{:S(2)}, u32[]{:S(2)}) collective-permute-start(bf16[2048,128]{0,1:T(8,128)(2,1)S(1)} %fusion.2), channel_id=1, source_target_pairs={{128,0},{129,1},{130,2},{131,3},{132,4},{133,5},{134,6},{135,7},{1... | collective-permute-start | bytes 1572872 | tf_op jit(solution)/shard_map/ppermute | solution.py:163
  281.4 17.2 %collective-permute-start.3 = (bf16[2048,128]{0,1:T(8,128)(2,1)S(1)}, bf16[2048,128]{0,1:T(8,128)(2,1)S(1)}, u32[]{:S(2)}, u32[]{:S(2)}) collective-permute-start(bf16[2048,128]{0,1:T(8,128)(2,1)S(1)} %bitcast.41), channel_id=1, source_target_pairs={{0,64},{1,65},{2,66},{3,67},{4,68},{5,69},{6,70},{7,71},{8,72},{9,... | collective-permute-start | bytes 1572872 | tf_op jit(solution)/shard_map/ppermute | solution.py:166
Sparse Core Ops, SparseCore 0:
  15.9 30.2 all-gather.2
  47.9 114.2 all-gather.4

commit v5 on v4

--- a/solution.py
+++ b/solution.py
@@ -31,12 +31,20 @@
     return out + jnp.einsum(eq, a_hi, b_lo, preferred_element_type=jnp.float32)
 
 
+def copy_kernel(t_ref, o_ref):
+    o_ref[0] = t_ref[...]
+
+
 def prepare(tile):
     n = tile.shape[0]
     nb = n // BLOCK
-    starts = jnp.arange(nb, dtype=jnp.int32) * BLOCK
-    blocks = jax.vmap(lambda s: lax.dynamic_slice(tile, (s, s), (BLOCK, BLOCK)))(starts)
-    blocks = blocks.astype(jnp.float32)
+    blocks = pl.pallas_call(
+        copy_kernel,
+        grid=(nb,),
+        in_specs=[pl.BlockSpec((BLOCK, BLOCK), lambda j: (j, j))],
+        out_specs=pl.BlockSpec((1, BLOCK, BLOCK), lambda j: (j, 0, 0)),
+        out_shape=jax.ShapeDtypeStruct((nb, BLOCK, BLOCK), tile.dtype),
+    )(tile).astype(jnp.float32)
     eye = jnp.eye(BLOCK, dtype=jnp.float32)
     diag = jnp.sum(blocks * eye[None], axis=2)
     lower = jnp.tril(jnp.ones((BLOCK, BLOCK), jnp.bool_), -1)
@@ -65,7 +73,7 @@
         v = v + jnp.dot(r_hi, p_lo, preferred_element_type=jnp.float32)
         v = v * d_ref[pl.ds(j, 1), :]
         v_hi, v_lo = split_bf16(v)
-        rows = f_ref[pl.ds(start, BLOCK), :]
+        rows = f_ref[pl.ds(start, BLOCK), : rest_ref.shape[1]]
         upd = jnp.dot(v_hi, rows, preferred_element_type=jnp.float32)
         upd = upd + jnp.dot(v_lo, rows, preferred_element_type=jnp.float32)
         rest_ref[...] = rest_ref[...] - upd
@@ -76,7 +84,7 @@
 
 
 def kernel_solve(tile, prod, inv_diag, rhs):
-    n = tile.shape[0]
+    n = rhs.shape[0]
     cols = rhs.shape[1]
     vmem = pl.BlockSpec(memory_space=pltpu.VMEM)
     out_t = pl.pallas_call(
@@ -134,14 +142,14 @@
     received = lax.all_to_all(outgoing, ("row", "col"), split_axis=0, concat_axis=0, tiled=True)
     slot_rows = received.reshape(tiles_block, tile_rows, columns)
     anc_values = slot_rows[block_owners].reshape(tiles_block * tile_rows, columns)
+    shard_rows, width = front.shape
     w_rows = anc_weight.shape[0]
-    both = jnp.concatenate([anc_weight, front], axis=0)
+    fold = shard_rows // w_rows
+    both = jnp.concatenate([front, anc_weight.reshape(shard_rows, width // fold)], axis=1)
     for axis in ("xh", "y", "z"):
         both = lax.all_gather(both, axis, axis=0, tiled=True)
-    both = both.reshape(-1, w_rows + front.shape[0], both.shape[1])
-    weight_tile = both[:, :w_rows].reshape(-1, both.shape[2])
-    front_tile = both[:, w_rows:].reshape(-1, both.shape[2])
-    width = front_tile.shape[1]
+    front_tile = both
+    weight_tile = both[:, width:].reshape(-1, w_rows, fold, width // fold).reshape(-1, width)
     anc_total = lax.dot_general(
         weight_tile, anc_values, (((0,), (0,)), ((), ())), preferred_element_type=jnp.float32
     )
@@ -158,7 +166,7 @@
     got_one = lax.ppermute(sol_one, "col", left)
     sol_one = jnp.where(col_index == 1, sol_one, got_one)
 
-    own_zero = (anc_total + split_dot_t(front_tile, sol_one.astype(jnp.float32))).astype(jnp.bfloat16)
+    own_zero = (anc_total + split_dot_t(front_tile[:, :width], sol_one.astype(jnp.float32))).astype(jnp.bfloat16)
     own_zero = jnp.where(row_index == 0, anc_total.astype(jnp.bfloat16), own_zero)
     other_zero = lax.ppermute(own_zero, "row", down)
     reduced_zero = rhs_values - own_zero.astype(jnp.float32) - other_zero.astype(jnp.float32)

time: 308 us -> 282 us (0.916)
  local copies, waits for them, and re-layouts: 63.7 us -> 11.9 us
  Pallas kernels: 19.7 us -> 35.8 us
  matrix products: 22.3 us -> 31.1 us
    gather x48 -> x0, local copies, waits for them, and re-layouts: 46.1 us -> none
    slice x1 -> x2, local copies, waits for them, and re-layouts: 8.38 us -> 0.01 us  [on_device(): both[:, width:].reshape(-1, w_rows, fold, width // fold).reshape(-1, width)]
    pallas_call x0 -> x1, Pallas kernels: none -> 8.26 us  [prepare(): pl.pallas_call(copy_kernel, grid=(nb,), in_specs=[pl.BlockSpec((BLOCK, BL...]
    pallas_call x2, Pallas kernels: 19.7 us -> 27.5 us  [kernel_solve(): pl.pallas_call(solve_kernel, out_shape=jax.ShapeDtypeStruct((cols, n), jn...]
    dot_general x1, matrix products: 1.44 us -> 4.88 us  [split_dot_t(): lax.dot_general(mat_bf16, hi, dims, preferred_element_type=jnp.float32)]
  transfers between devices with their start and end apart: 7 -> 7, of which waited for: 6 -> 5; matrix products, arithmetic and copies ran while one was open for 6% -> 4% of each run, Pallas kernels for 0% -> 0%
where the time goes in v5:
time: 282 us; the launch traced here: 280 us
  waiting for transfers between devices  162 us (57%)
  Pallas kernels  35.8 us (13%)
  matrix products  31.1 us (11%)
  between operations  13.9 us (5%)
  starting transfers between devices  12.1 us (4%)
  local copies, waits for them, and re-layouts  11.9 us (4%)
  blocking collectives  8.21 us (3%)
  other arithmetic  4.76 us (2%)
    all_gather x2, waiting for transfers between devices, on_device(): both = lax.all_gather(both, axis, axis=0, tiled=True)  134 us
    pallas_call x2, Pallas kernels, kernel_solve(): pl.pallas_call(solve_kernel, out_shape=jax.ShapeDtypeStruct((cols, n), jn...  27.5 us
    ppermute x1, waiting for transfers between devices, on_device(): got_zero = lax.ppermute(sol_zero, 'col', right)  15.9 us
    ppermute x1, waiting for transfers between devices, on_device(): got_one = lax.ppermute(sol_one, 'col', left)  10.3 us
    pallas_call x1, Pallas kernels, prepare(): pl.pallas_call(copy_kernel, grid=(nb,), in_specs=[pl.BlockSpec((BLOCK, BL...  8.26 us
    all_gather x1, blocking collectives, on_device(): both = lax.all_gather(both, axis, axis=0, tiled=True)  8.21 us
    dot_general x12, matrix products, mm3(): out = out + jnp.einsum(eq, a_lo, b_hi, preferred_element_type=jnp.float32)  6.52 us
    dot_general x12, matrix products, mm3(): return out + jnp.einsum(eq, a_hi, b_lo, preferred_element_type=jnp.float32)  6.23 us
  transfers between devices with their start and end apart: 7, of which 5 were waited for; matrix products, arithmetic and copies ran while one was open for 4% of the time, Pallas kernels for 0%

profile of v5, /device:TPU:6, one launch (start us, length us, event | category | flops | bytes accessed | tf_op | source)
XLA Modules:
  0.0 280.0 jit_solution(2666645825678966263)
XLA Ops:
  6.5 0.8 reshape.122
  7.4 0.9 pad_maximum_fusion
  8.3 8.2 %all_gather.9 = bf16[64,2560]{1,0:T(8,128)(2,1)} all-gather(bf16[32,2560]{1,0:T(8,128)(2,1)S(1)} %pad_maximum_fusion), channel_id=1, replica_groups=mesh['row'=2,'col'=2,'z'=8,'y'=4,'xh'=2] {'xh'}, dimensions={0}, use_global_device_ids=true | all-gather | bytes 491520 | tf_op jit(solution)/shard_map/all_gather | solution.py:150
  16.6 30.4 %all-gather.3.cloned.1.call-done = bf16[256,2560]{1,0:T(8,128)(2,1)} async-done(((bf16[64,2560]{1,0:T(8,128)(2,1)}), bf16[256,2560]{1,0:T(8,128)(2,1)}) %all-gather.3.cloned.1.call-update) | async-done | bytes 1310736 | tf_op jit(solution)/shard_map/all_gather | solution.py:150
  47.0 0.7 broadcast_compare_fusion
  47.9 1.2 gather_fusion.1
  49.1 1.3 gather_fusion
  50.4 0.9 gather_fusion.2
  51.5 0.7 broadcast_in_dim.28
  52.1 4.1 %all-to-all-start = ((bf16[4,128,128]{2,1,0:T(8,128)(2,1)}), bf16[4,128,128]{2,1,0:T(8,128)(2,1)S(1)}, u32[]{:S(2)}, u32[]{:S(2)}) async-start(bf16[4,128,128]{2,1,0:T(8,128)(2,1)} %bitcast.5), calls=%async_computation | async-start | bytes 262144 | tf_op jit(solution)/shard_map/all_to_all | solution.py:142
  56.3 2.0 copy.14
  58.3 0.7 compare_select_fusion.1
  59.2 0.6 gather_fusion.3
  59.8 103.3 %all-gather.5.cloned.1.call-done.t_ref.f_ref = bf16[2048,2560]{1,0:T(8,128)(2,1)} async-done(((bf16[256,2560]{1,0:T(8,128)(2,1)}), bf16[2048,2560]{1,0:T(8,128)(2,1)}) %all-gather.5.cloned.1.call-update) | async-done | bytes 10485776 | tf_op jit(solution)/shard_map/all_gather | solution.py:150
  163.1 8.3 %shard_map.73 = bf16[16,128,128]{2,1,0:T(8,128)(2,1)} custom-call(bf16[2048,2560]{1,0:T(8,128)(2,1)} %all-gather.5.cloned.1.call-done.t_ref.f_ref), custom_call_target="tpu_custom_call" | custom-call | tf_op jit(solution)/shard_map/pallas_call | solution.py:41
  171.3 1.5 fusion.17
  172.8 2.0 fusion.31
  174.8 2.0 convolution_add_fusion.23
  176.9 0.9 convolution_add_fusion.22
  177.7 0.5 fusion.53
  178.5 0.5 convolution_add_fusion.21
  179.0 0.5 convolution_add_fusion.20
  180.5 0.3 fusion.54
  181.1 0.3 convolution_add_fusion.16
  182.3 0.3 fusion.55
  182.9 0.3 convolution_add_fusion.12
  184.1 0.3 fusion.56
  184.7 0.3 convolution_add_fusion.8
  186.5 0.3 convolution_add_fusion.4
  187.2 0.3 fusion.16
  187.5 0.3 fusion.62
  187.8 0.7 copy-done.1
  188.5 1.3 convolution_add_fusion.1
  189.8 2.6 reshape_reshape.3
  192.3 3.2 %fusion.85 = (bf16[2048,128]{0,1:T(8,128)(2,1)S(1)}, f32[2048,128]{0,1:T(8,128)}) fusion(bf16[512,2048]{1,0:T(8,128)(2,1)} %reshape_reshape.3, bf16[512,128]{1,0:T(8,128)(2,1)S(1)} %bitcast.24), kind=kOutput, calls=%fused_computation.146 | convolution fusion | flops 268697600 | bytes 3801088 | tf_op jit(solution)/shard_map/dot_general | solution.py:153
  195.5 1.6 collective-permute-start
  197.1 2.1 convolution_add_fusion.p_ref
  199.5 13.7 %shard_map.74 = bf16[128,2048]{1,0:T(8,128)(2,1)S(1)} custom-call(bf16[2048,2560]{1,0:T(8,128)(2,1)} %all-gather.5.cloned.1.call-done.t_ref.f_ref, f32[16,128,128]{2,1,0:T(8,128)S(1)} %convolution_add_fusion.p_ref, f32[16,128]{1,0:T(8,128)S(1)} %broadcast_divide_fusion.d_ref, f32[128,2048]{1,0:T(8,128)S(1)} %fusion.20.r_ref), custom_call_target="tpu_custom_call" | custom-call | tf_op jit(solution)/shard_map/pallas_call | solution.py:90
  213.3 3.7 %collective-permute-start.1 = (bf16[2048,128]{0,1:T(8,128)(2,1)S(1)}, bf16[2048,128]{0,1:T(8,128)(2,1)}, u32[]{:S(2)}, u32[]{:S(2)}) collective-permute-start(bf16[2048,128]{0,1:T(8,128)(2,1)S(1)} %bitcast.22), channel_id=1, source_target_pairs={{64,0},{65,1},{66,2},{67,3},{68,4},{69,5},{70,6},{71,7},{72,8},{73... | collective-permute-start | bytes 1572872 | tf_op jit(solution)/shard_map/ppermute | solution.py:166
  217.0 10.3 %collective-permute-done.1 = bf16[2048,128]{0,1:T(8,128)(2,1)} collective-permute-done((bf16[2048,128]{0,1:T(8,128)(2,1)S(1)}, bf16[2048,128]{0,1:T(8,128)(2,1)}, u32[]{:S(2)}, u32[]{:S(2)}) %collective-permute-start.1) | collective-permute-done | bytes 524320 | tf_op jit(solution)/shard_map/ppermute | solution.py:166
  227.3 4.8 %fusion.2 = f32[2048,128]{0,1:T(8,128)S(1)} fusion(bf16[2048,2560]{1,0:T(8,128)(2,1)} %all-gather.5.cloned.1.call-done.t_ref.f_ref, bf16[2048,128]{0,1:T(8,128)(2,1)S(1)} %broadcast_select_fusion), kind=kOutput, calls=%fused_computation.6 | convolution fusion | flops 1074528256 | bytes 9961472 | tf_op jit(solution)/shard_map/dot_general | solution.py:17
  232.2 4.9 %fusion.13 = bf16[2048,128]{0,1:T(8,128)(2,1)S(1)} fusion(bf16[2048,128]{0,1:T(8,128)(2,1)S(1)} %copy-done.5, f32[2048,128]{0,1:T(8,128)S(1)} %copy-done.6, f32[2048,128]{0,1:T(8,128)S(1)} %fusion.2, bf16[2048,128]{0,1:T(8,128)(2,1)S(1)} %broadcast_select_fusion, bf16[2048,2560]{1,0:T(8,128)(2,1)} %all-gather.5.cloned.1.call-done.t_ref.f_ref, pred[]{:T(512)S(6)} %eq.49), kind=kOutput, calls=%fused_computation.11 | convolution fusion | flops 1074790400 | bytes 12058625 | tf_op jit(solution)/shard_map/dot_general | solution.py:16
  237.1 1.3 collective-permute-start.2
  238.4 2.5 collective-permute-done.2
  241.1 13.7 %shard_map.75 = bf16[128,2048]{1,0:T(8,128)(2,1)S(1)} custom-call(bf16[2048,2560]{1,0:T(8,128)(2,1)} %all-gather.5.cloned.1.call-done.t_ref.f_ref, f32[16,128,128]{2,1,0:T(8,128)S(1)} %convolution_add_fusion.p_ref, f32[16,128]{1,0:T(8,128)S(1)} %broadcast_divide_fusion.d_ref, f32[128,2048]{1,0:T(8,128)S(1)} %fusion.22.r_ref), custom_call_target="tpu_custom_call" | custom-call | tf_op jit(solution)/shard_map/pallas_call | solution.py:90
  254.9 1.3 collective-permute-start.3
  256.2 15.9 %collective-permute-done.3 = bf16[2048,128]{0,1:T(8,128)(2,1)S(1)} collective-permute-done((bf16[2048,128]{0,1:T(8,128)(2,1)S(1)}, bf16[2048,128]{0,1:T(8,128)(2,1)S(1)}, u32[]{:S(2)}, u32[]{:S(2)}) %collective-permute-start.3) | collective-permute-done | bytes 524320 | tf_op jit(solution)/shard_map/ppermute | solution.py:174
  272.1 1.0 copy.19
  (62 shorter events, 6.8 us)
Async XLA Ops:
  6.5 43.9 %copy-start = (bf16[512,128]{1,0:T(8,128)(2,1)S(1)}, bf16[512,128]{1,0:T(8,128)(2,1)}, u32[]{:S(2)}) copy-start(bf16[512,128]{1,0:T(8,128)(2,1)} %param.9) | copy-start | bytes 393220
  6.5 40.4 %all-gather.3.cloned.1.call-start = ((), (), s32[]{:S(2)}) async-start(), calls=%async_computation.1 | async-start | bytes 1638400 | tf_op jit(solution)/shard_map/all_gather | solution.py:150
  16.5 146.5 %all-gather.5.cloned.1.call-start = ((), (), s32[]{:S(2)}) async-start(), calls=%async_computation.2 | async-start | bytes 11796480 | tf_op jit(solution)/shard_map/all_gather | solution.py:150
  52.1 7.0 %all-to-all-start = ((bf16[4,128,128]{2,1,0:T(8,128)(2,1)}), bf16[4,128,128]{2,1,0:T(8,128)(2,1)S(1)}, u32[]{:S(2)}, u32[]{:S(2)}) async-start(bf16[4,128,128]{2,1,0:T(8,128)(2,1)} %bitcast.5), calls=%async_computation | async-start | bytes 262144 | tf_op jit(solution)/shard_map/all_to_all | solution.py:142
  171.3 5.5 %copy-start.9 = (bf16[16,128,128]{2,1,0:T(8,128)(2,1)S(1)}, bf16[16,128,128]{2,1,0:T(8,128)(2,1)}, u32[]{:S(2)}) copy-start(bf16[16,128,128]{2,1,0:T(8,128)(2,1)} %shard_map.73) | copy-start | bytes 1572868
  187.1 2.6 slice-start
  187.5 1.0 copy-start.1
  192.3 6.9 %copy-start.2 = (bf16[2048,128]{0,1:T(8,128)(2,1)S(1)}, bf16[2048,128]{0,1:T(8,128)(2,1)}, u32[]{:S(2)}) copy-start(bf16[2048,128]{0,1:T(8,128)(2,1)} %copy.14) | copy-start | bytes 1572868
  195.5 17.8 %copy-start.4 = (bf16[2048,128]{0,1:T(8,128)(2,1)}, bf16[2048,128]{0,1:T(8,128)(2,1)S(1)}, u32[]{:S(2)}) copy-start(bf16[2048,128]{0,1:T(8,128)(2,1)S(1)} %get-tuple-element.5) | copy-start | bytes 1572868
  195.5 3.8 %collective-permute-start = (bf16[2048,128]{0,1:T(8,128)(2,1)S(1)}, bf16[2048,128]{0,1:T(8,128)(2,1)S(1)}, u32[]{:S(2)}, u32[]{:S(2)}) collective-permute-start(bf16[2048,128]{0,1:T(8,128)(2,1)S(1)} %get-tuple-element.5), channel_id=1, source_target_pairs={{0,128},{1,129},{2,130},{3,131},{4,132},{5,133},{6,134},{7,135},{8... | collective-permute-start | bytes 1572872 | tf_op jit(solution)/shard_map/ppermute | solution.py:163
  213.3 18.9 %copy-start.6 = (f32[2048,128]{0,1:T(8,128)S(1)}, f32[2048,128]{0,1:T(8,128)}, u32[]{:S(2)}) copy-start(f32[2048,128]{0,1:T(8,128)} %get-tuple-element.6) | copy-start | bytes 3145732
  213.3 18.9 %copy-start.5 = (bf16[2048,128]{0,1:T(8,128)(2,1)S(1)}, bf16[2048,128]{0,1:T(8,128)(2,1)}, u32[]{:S(2)}) copy-start(bf16[2048,128]{0,1:T(8,128)(2,1)} %copy-done.4) | copy-start | bytes 1572868
  213.3 13.9 %collective-permute-start.1 = (bf16[2048,128]{0,1:T(8,128)(2,1)S(1)}, bf16[2048,128]{0,1:T(8,128)(2,1)}, u32[]{:S(2)}, u32[]{:S(2)}) collective-permute-start(bf16[2048,128]{0,1:T(8,128)(2,1)S(1)} %bitcast.22), channel_id=1, source_target_pairs={{64,0},{65,1},{66,2},{67,3},{68,4},{69,5},{70,6},{71,7},{72,8},{73... | collective-permute-start | bytes 1572872 | tf_op jit(solution)/shard_map/ppermute | solution.py:166
  227.3 9.8 %copy-start.7 = (bf16[2048,128]{0,1:T(8,128)(2,1)}, bf16[2048,128]{0,1:T(8,128)(2,1)S(1)}, u32[]{:S(2)}) copy-start(bf16[2048,128]{0,1:T(8,128)(2,1)S(1)} %broadcast_select_fusion) | copy-start | bytes 1572868
  232.1 8.7 %copy-start.3 = (bf16[2048,128]{0,1:T(8,128)(2,1)S(1)}, bf16[2048,128]{0,1:T(8,128)(2,1)}, u32[]{:S(2)}) copy-start(bf16[2048,128]{0,1:T(8,128)(2,1)} %copy.14) | copy-start | bytes 1572868
  237.1 3.8 %collective-permute-start.2 = (bf16[2048,128]{0,1:T(8,128)(2,1)S(1)}, bf16[2048,128]{0,1:T(8,128)(2,1)S(1)}, u32[]{:S(2)}, u32[]{:S(2)}) collective-permute-start(bf16[2048,128]{0,1:T(8,128)(2,1)S(1)} %fusion.13), channel_id=1, source_target_pairs={{128,0},{129,1},{130,2},{131,3},{132,4},{133,5},{134,6},{135,7},{1... | collective-permute-start | bytes 1572872 | tf_op jit(solution)/shard_map/ppermute | solution.py:171
  238.4 33.7 %copy-start.8 = (bf16[2048,128]{0,1:T(8,128)(2,1)S(1)}, bf16[2048,128]{0,1:T(8,128)(2,1)}, u32[]{:S(2)}) copy-start(bf16[2048,128]{0,1:T(8,128)(2,1)} %copy-done.7) | copy-start | bytes 1572868
  254.9 17.2 %collective-permute-start.3 = (bf16[2048,128]{0,1:T(8,128)(2,1)S(1)}, bf16[2048,128]{0,1:T(8,128)(2,1)S(1)}, u32[]{:S(2)}, u32[]{:S(2)}) collective-permute-start(bf16[2048,128]{0,1:T(8,128)(2,1)S(1)} %bitcast.23), channel_id=1, source_target_pairs={{0,64},{1,65},{2,66},{3,67},{4,68},{5,69},{6,70},{7,71},{8,72},{9,... | collective-permute-start | bytes 1572872 | tf_op jit(solution)/shard_map/ppermute | solution.py:174
Sparse Core Ops, SparseCore 0:
  16.6 30.2 all-gather.2
  48.7 114.2 all-gather.4

commit v6 on v5

--- a/solution.py
+++ b/solution.py
@@ -31,19 +31,29 @@
     return out + jnp.einsum(eq, a_hi, b_lo, preferred_element_type=jnp.float32)
 
 
-def copy_kernel(t_ref, o_ref):
-    o_ref[0] = t_ref[...]
+def diag_kernel(t_hbm, o_ref, sems):
+    nb = o_ref.shape[0]
+    copies = [
+        pltpu.make_async_copy(
+            t_hbm.at[pl.ds(j * BLOCK, BLOCK), pl.ds(j * BLOCK, BLOCK)], o_ref.at[j], sems.at[j]
+        )
+        for j in range(nb)
+    ]
+    for one in copies:
+        one.start()
+    for one in copies:
+        one.wait()
 
 
 def prepare(tile):
     n = tile.shape[0]
     nb = n // BLOCK
     blocks = pl.pallas_call(
-        copy_kernel,
-        grid=(nb,),
-        in_specs=[pl.BlockSpec((BLOCK, BLOCK), lambda j: (j, j))],
-        out_specs=pl.BlockSpec((1, BLOCK, BLOCK), lambda j: (j, 0, 0)),
+        diag_kernel,
+        in_specs=[pl.BlockSpec(memory_space=pl.ANY)],
+        out_specs=pl.BlockSpec(memory_space=pltpu.VMEM),
         out_shape=jax.ShapeDtypeStruct((nb, BLOCK, BLOCK), tile.dtype),
+        scratch_shapes=[pltpu.SemaphoreType.DMA((nb,))],
     )(tile).astype(jnp.float32)
     eye = jnp.eye(BLOCK, dtype=jnp.float32)
     diag = jnp.sum(blocks * eye[None], axis=2)
@@ -146,8 +156,10 @@
     w_rows = anc_weight.shape[0]
     fold = shard_rows // w_rows
     both = jnp.concatenate([front, anc_weight.reshape(shard_rows, width // fold)], axis=1)
-    for axis in ("xh", "y", "z"):
+    for axis in ("xh", "z", "y"):
         both = lax.all_gather(both, axis, axis=0, tiled=True)
+    n_y, n_z = lax.axis_size("y"), lax.axis_size("z")
+    both = both.reshape(n_y, n_z, -1, both.shape[1]).transpose(1, 0, 2, 3).reshape(-1, both.shape[1])
     front_tile = both
     weight_tile = both[:, width:].reshape(-1, w_rows, fold, width // fold).reshape(-1, width)
     anc_total = lax.dot_general(
@@ -166,7 +178,10 @@
     got_one = lax.ppermute(sol_one, "col", left)
     sol_one = jnp.where(col_index == 1, sol_one, got_one)
 
-    own_zero = (anc_total + split_dot_t(front_tile[:, :width], sol_one.astype(jnp.float32))).astype(jnp.bfloat16)
+    front_term = lax.dot_general(
+        front_tile[:, :width], sol_one, (((0,), (0,)), ((), ())), preferred_element_type=jnp.float32
+    )
+    own_zero = (anc_total + front_term).astype(jnp.bfloat16)
     own_zero = jnp.where(row_index == 0, anc_total.astype(jnp.bfloat16), own_zero)
     other_zero = lax.ppermute(own_zero, "row", down)
     reduced_zero = rhs_values - own_zero.astype(jnp.float32) - other_zero.astype(jnp.float32)

time: 282 us -> 283 us (level)
  local copies, waits for them, and re-layouts: 11.9 us -> 24.5 us
  matrix products: 31.1 us -> 24.7 us
  Pallas kernels: 35.8 us -> 29.5 us
    reshape x0 -> x1, local copies, waits for them, and re-layouts: none -> 9.05 us  [on_device(): both.reshape(n_y, n_z, -1, both.shape[1]).transpose(1, 0, 2, 3)]
    pallas_call x1, Pallas kernels: 8.26 us -> 1.94 us  [prepare(): pl.pallas_call(diag_kernel, in_specs=[pl.BlockSpec(memory_space=pl.ANY)],...]
    dot_general x2 -> x1, matrix products: 9.71 us -> 4.81 us  [on_device(): lax.dot_general(front_tile[:, :width], sol_one, (((0,), (0,)), ((), ())),...]
    slice x2 -> x1, local copies, waits for them, and re-layouts: 0.01 us -> 3.07 us  [on_device(): both[:, width:].reshape(-1, w_rows, fold, width // fold).reshape(-1, width)]
where the time goes in v6:
time: 283 us; the launch traced here: 281 us
  waiting for transfers between devices  164 us (58%)
  Pallas kernels  29.5 us (10%)
  matrix products  24.7 us (9%)
  local copies, waits for them, and re-layouts  24.5 us (9%)
  between operations  13.9 us (5%)
  starting transfers between devices  12.1 us (4%)
  blocking collectives  8.21 us (3%)
  other arithmetic  4.7 us (2%)
    all_gather x2, waiting for transfers between devices, on_device(): both = lax.all_gather(both, axis, axis=0, tiled=True)  136 us
    pallas_call x2, Pallas kernels, kernel_solve(): pl.pallas_call(solve_kernel, out_shape=jax.ShapeDtypeStruct((cols, n), jn...  27.6 us
    ppermute x1, waiting for transfers between devices, on_device(): got_zero = lax.ppermute(sol_zero, 'col', right)  14.9 us
    ppermute x1, waiting for transfers between devices, on_device(): got_one = lax.ppermute(sol_one, 'col', left)  10.4 us
    reshape x1, local copies, waits for them, and re-layouts, on_device(): both.reshape(n_y, n_z, -1, both.shape[1]).transpose(1, 0, 2, 3)  9.05 us
    all_gather x1, blocking collectives, on_device(): both = lax.all_gather(both, axis, axis=0, tiled=True)  8.21 us
    dot_general x12, matrix products, mm3(): out = out + jnp.einsum(eq, a_lo, b_hi, preferred_element_type=jnp.float32)  6.73 us
    dot_general x12, matrix products, mm3(): return out + jnp.einsum(eq, a_hi, b_lo, preferred_element_type=jnp.float32)  6.11 us
  transfers between devices with their start and end apart: 7, of which 5 were waited for; matrix products, arithmetic and copies ran while one was open for 4% of the time, Pallas kernels for 0%

profile of v6, /device:TPU:6, one launch (start us, length us, event | category | flops | bytes accessed | tf_op | source)
XLA Modules:
  0.0 281.5 jit_solution(3334531226500605322)
XLA Ops:
  6.5 0.8 reshape.128
  7.4 0.9 pad_maximum_fusion
  8.3 8.2 %all_gather.9 = bf16[64,2560]{1,0:T(8,128)(2,1)} all-gather(bf16[32,2560]{1,0:T(8,128)(2,1)S(1)} %pad_maximum_fusion), channel_id=1, replica_groups=mesh['row'=2,'col'=2,'z'=8,'y'=4,'xh'=2] {'xh'}, dimensions={0}, use_global_device_ids=true | all-gather | bytes 491520 | tf_op jit(solution)/shard_map/all_gather | solution.py:160
  16.6 45.1 %all-gather.3.cloned.1.call-done = bf16[512,2560]{1,0:T(8,128)(2,1)} async-done(((bf16[64,2560]{1,0:T(8,128)(2,1)}), bf16[512,2560]{1,0:T(8,128)(2,1)}) %all-gather.3.cloned.1.call-update) | async-done | bytes 2621456 | tf_op jit(solution)/shard_map/all_gather | solution.py:160
  61.7 0.7 broadcast_compare_fusion
  62.6 1.2 gather_fusion.1
  63.9 1.3 gather_fusion
  65.2 0.9 gather_fusion.2
  66.2 0.7 broadcast_in_dim.28
  66.9 4.1 %all-to-all-start = ((bf16[4,128,128]{2,1,0:T(8,128)(2,1)}), bf16[4,128,128]{2,1,0:T(8,128)(2,1)S(1)}, u32[]{:S(2)}, u32[]{:S(2)}) async-start(bf16[4,128,128]{2,1,0:T(8,128)(2,1)} %bitcast.9), calls=%async_computation | async-start | bytes 262144 | tf_op jit(solution)/shard_map/all_to_all | solution.py:152
  71.0 2.0 copy.15
  73.1 0.7 compare_select_fusion.1
  73.9 0.6 gather_fusion.3
  74.5 90.9 %all-gather.5.cloned.1.call-done = bf16[2048,2560]{1,0:T(8,128)(2,1)} async-done(((bf16[512,2560]{1,0:T(8,128)(2,1)}), bf16[2048,2560]{1,0:T(8,128)(2,1)}) %all-gather.5.cloned.1.call-update) | async-done | bytes 10485776 | tf_op jit(solution)/shard_map/all_gather | solution.py:160
  165.4 9.0 %copy.14 = bf16[4,8,64,2560]{3,2,0,1:T(8,128)(2,1)} copy(bf16[4,8,64,2560]{3,2,1,0:T(8,128)(2,1)} %bitcast.36) | data formatting | bytes 20971520 | tf_op jit(solution)/shard_map/reshape | solution.py:162
  174.5 1.9 shard_map.73
  176.4 1.4 fusion.12
  177.9 2.1 fusion.26
  180.0 2.2 convolution_add_fusion.23
  182.2 0.9 convolution_add_fusion.22
  183.4 0.5 fusion.48
  183.9 3.1 %slice.16 = bf16[2048,512]{1,0:T(8,128)(2,1)} slice(bf16[2048,2560]{1,0:T(8,128)(2,1)} %bitcast.32), slice={[0:2048], [2048:2560]} | slice | bytes 4194304 | tf_op jit(solution)/shard_map/slice | solution.py:164
  191.1 0.5 convolution_add_fusion.21
  191.7 0.5 convolution_add_fusion.20
  192.2 0.3 fusion.49
  192.5 0.3 convolution_add_fusion.17
  192.9 0.3 convolution_add_fusion.16
  193.2 0.3 fusion.50
  194.4 0.3 convolution_add_fusion.9
  194.7 0.3 convolution_add_fusion.8
  195.6 0.5 convolution_add_fusion.4
  196.1 0.3 fusion.58
  196.5 0.6 copy-done.2
  197.1 1.3 convolution_add_fusion.1
  198.4 3.1 %reshape_reshape.3 = bf16[512,2048]{1,0:T(8,128)(2,1)S(1)} reshape(bf16[2048,512]{1,0:T(8,128)(2,1)} %slice.16) | data formatting | bytes 4194304 | tf_op jit(solution)/shard_map/reshape;reshape | solution.py:164
  201.6 1.5 fusion.81
  203.0 1.6 collective-permute-start
  204.6 1.8 convolution_add_fusion.p_ref
  206.7 13.8 %shard_map.74 = bf16[128,2048]{1,0:T(8,128)(2,1)S(1)} custom-call(bf16[2048,2560]{1,0:T(8,128)(2,1)} %bitcast.33, f32[16,128,128]{2,1,0:T(8,128)S(1)} %convolution_add_fusion.p_ref, f32[16,128]{1,0:T(8,128)S(1)} %broadcast_divide_fusion.d_ref, f32[128,2048]{1,0:T(8,128)S(1)} %fusion.15.r_ref), custom_call_target="tpu_custom_call" | custom-call | tf_op jit(solution)/shard_map/pallas_call | solution.py:100
  220.6 3.7 %collective-permute-start.1 = (bf16[2048,128]{0,1:T(8,128)(2,1)S(1)}, bf16[2048,128]{0,1:T(8,128)(2,1)}, u32[]{:S(2)}, u32[]{:S(2)}) collective-permute-start(bf16[2048,128]{0,1:T(8,128)(2,1)S(1)} %bitcast.29), channel_id=1, source_target_pairs={{64,0},{65,1},{66,2},{67,3},{68,4},{69,5},{70,6},{71,7},{72,8},{73... | collective-permute-start | bytes 1572872 | tf_op jit(solution)/shard_map/ppermute | solution.py:178
  224.3 10.4 %collective-permute-done.1 = bf16[2048,128]{0,1:T(8,128)(2,1)} collective-permute-done((bf16[2048,128]{0,1:T(8,128)(2,1)S(1)}, bf16[2048,128]{0,1:T(8,128)(2,1)}, u32[]{:S(2)}, u32[]{:S(2)}) %collective-permute-start.1) | collective-permute-done | bytes 524320 | tf_op jit(solution)/shard_map/ppermute | solution.py:178
  234.7 4.8 %fusion.8 = bf16[2048,128]{0,1:T(8,128)(2,1)S(1)} fusion(bf16[2048,128]{0,1:T(8,128)(2,1)} %copy-done.5, f32[2048,128]{0,1:T(8,128)S(1)} %copy-done.6, bf16[2048,2560]{1,0:T(8,128)(2,1)} %bitcast.34, pred[]{:T(512)S(6)} %eq.49, bf16[2048,128]{0,1:T(8,128)(2,1)} %collective-permute-done.1, pred[]{:T(512)S(6)} %eq.43, bf16[128,2048]{1,0:T(8,128)(2,1)S(1)} %shard_map.74), kind=kOutput, calls=%fused_computation.8 | convolution fusion | flops 1074790400 | bytes 11534338 | tf_op jit(solution)/shard_map/dot_general | solution.py:181
  239.5 1.3 collective-permute-start.2
  240.8 2.5 collective-permute-done.2
  243.6 13.8 %shard_map.75 = bf16[128,2048]{1,0:T(8,128)(2,1)S(1)} custom-call(bf16[2048,2560]{1,0:T(8,128)(2,1)} %bitcast.35, f32[16,128,128]{2,1,0:T(8,128)S(1)} %convolution_add_fusion.p_ref, f32[16,128]{1,0:T(8,128)S(1)} %broadcast_divide_fusion.d_ref, f32[128,2048]{1,0:T(8,128)S(1)} %fusion.17.r_ref), custom_call_target="tpu_custom_call" | custom-call | tf_op jit(solution)/shard_map/pallas_call | solution.py:100
  257.4 1.3 collective-permute-start.3
  258.7 14.9 %collective-permute-done.3 = bf16[2048,128]{0,1:T(8,128)(2,1)S(1)} collective-permute-done((bf16[2048,128]{0,1:T(8,128)(2,1)S(1)}, bf16[2048,128]{0,1:T(8,128)(2,1)S(1)}, u32[]{:S(2)}, u32[]{:S(2)}) %collective-permute-start.3) | collective-permute-done | bytes 524320 | tf_op jit(solution)/shard_map/ppermute | solution.py:189
  273.6 1.0 copy.19
  (56 shorter events, 7.0 us)
Async XLA Ops:
  6.5 58.6 %copy-start = (bf16[512,128]{1,0:T(8,128)(2,1)S(1)}, bf16[512,128]{1,0:T(8,128)(2,1)}, u32[]{:S(2)}) copy-start(bf16[512,128]{1,0:T(8,128)(2,1)} %param.9) | copy-start | bytes 393220
  6.5 55.2 %all-gather.3.cloned.1.call-start = ((), (), s32[]{:S(2)}) async-start(), calls=%async_computation.1 | async-start | bytes 2949120 | tf_op jit(solution)/shard_map/all_gather | solution.py:160
  16.5 148.9 %all-gather.5.cloned.1.call-start = ((), (), s32[]{:S(2)}) async-start(), calls=%async_computation.2 | async-start | bytes 13107200 | tf_op jit(solution)/shard_map/all_gather | solution.py:160
  66.9 7.0 %all-to-all-start = ((bf16[4,128,128]{2,1,0:T(8,128)(2,1)}), bf16[4,128,128]{2,1,0:T(8,128)(2,1)S(1)}, u32[]{:S(2)}, u32[]{:S(2)}) async-start(bf16[4,128,128]{2,1,0:T(8,128)(2,1)} %bitcast.9), calls=%async_computation | async-start | bytes 262144 | tf_op jit(solution)/shard_map/all_to_all | solution.py:152
  176.4 5.8 %copy-start.7 = (bf16[16,128,128]{2,1,0:T(8,128)(2,1)S(1)}, bf16[16,128,128]{2,1,0:T(8,128)(2,1)}, u32[]{:S(2)}) copy-start(bf16[16,128,128]{2,1,0:T(8,128)(2,1)} %shard_map.73) | copy-start | bytes 1572868
  196.1 1.0 copy-start.2
  201.5 4.9 %copy-start.3 = (bf16[2048,128]{0,1:T(8,128)(2,1)S(1)}, bf16[2048,128]{0,1:T(8,128)(2,1)}, u32[]{:S(2)}) copy-start(bf16[2048,128]{0,1:T(8,128)(2,1)} %copy.15) | copy-start | bytes 1572868
  203.0 17.5 %copy-start.5 = (bf16[2048,128]{0,1:T(8,128)(2,1)}, bf16[2048,128]{0,1:T(8,128)(2,1)S(1)}, u32[]{:S(2)}) copy-start(bf16[2048,128]{0,1:T(8,128)(2,1)S(1)} %get-tuple-element.5) | copy-start | bytes 1572868
  203.0 3.5 %collective-permute-start = (bf16[2048,128]{0,1:T(8,128)(2,1)S(1)}, bf16[2048,128]{0,1:T(8,128)(2,1)S(1)}, u32[]{:S(2)}, u32[]{:S(2)}) collective-permute-start(bf16[2048,128]{0,1:T(8,128)(2,1)S(1)} %get-tuple-element.5), channel_id=1, source_target_pairs={{0,128},{1,129},{2,130},{3,131},{4,132},{5,133},{6,134},{7,135},{8... | collective-permute-start | bytes 1572872 | tf_op jit(solution)/shard_map/ppermute | solution.py:175
  206.5 28.2 %copy-start.6 = (f32[2048,128]{0,1:T(8,128)S(1)}, f32[2048,128]{0,1:T(8,128)}, u32[]{:S(2)}) copy-start(f32[2048,128]{0,1:T(8,128)} %get-tuple-element.6) | copy-start | bytes 3145732
  220.5 22.8 %copy-start.4 = (bf16[2048,128]{0,1:T(8,128)(2,1)S(1)}, bf16[2048,128]{0,1:T(8,128)(2,1)}, u32[]{:S(2)}) copy-start(bf16[2048,128]{0,1:T(8,128)(2,1)} %copy.15) | copy-start | bytes 1572868
  220.6 14.2 %collective-permute-start.1 = (bf16[2048,128]{0,1:T(8,128)(2,1)S(1)}, bf16[2048,128]{0,1:T(8,128)(2,1)}, u32[]{:S(2)}, u32[]{:S(2)}) collective-permute-start(bf16[2048,128]{0,1:T(8,128)(2,1)S(1)} %bitcast.29), channel_id=1, source_target_pairs={{64,0},{65,1},{66,2},{67,3},{68,4},{69,5},{70,6},{71,7},{72,8},{73... | collective-permute-start | bytes 1572872 | tf_op jit(solution)/shard_map/ppermute | solution.py:178
  239.5 3.8 %collective-permute-start.2 = (bf16[2048,128]{0,1:T(8,128)(2,1)S(1)}, bf16[2048,128]{0,1:T(8,128)(2,1)S(1)}, u32[]{:S(2)}, u32[]{:S(2)}) collective-permute-start(bf16[2048,128]{0,1:T(8,128)(2,1)S(1)} %fusion.8), channel_id=1, source_target_pairs={{128,0},{129,1},{130,2},{131,3},{132,4},{133,5},{134,6},{135,7},{1... | collective-permute-start | bytes 1572872 | tf_op jit(solution)/shard_map/ppermute | solution.py:186
  243.3 31.3 %copy-start.1 = (bf16[512,128]{1,0:T(8,128)(2,1)S(1)}, bf16[512,128]{1,0:T(8,128)(2,1)}, u32[]{:S(2)}) copy-start(bf16[512,128]{1,0:T(8,128)(2,1)} %param.9) | copy-start | bytes 393220
  257.4 16.2 %collective-permute-start.3 = (bf16[2048,128]{0,1:T(8,128)(2,1)S(1)}, bf16[2048,128]{0,1:T(8,128)(2,1)S(1)}, u32[]{:S(2)}, u32[]{:S(2)}) collective-permute-start(bf16[2048,128]{0,1:T(8,128)(2,1)S(1)} %bitcast.30), channel_id=1, source_target_pairs={{0,64},{1,65},{2,66},{3,67},{4,68},{5,69},{6,70},{7,71},{8,72},{9,... | collective-permute-start | bytes 1572872 | tf_op jit(solution)/shard_map/ppermute | solution.py:189
Sparse Core Ops, SparseCore 0:
  16.6 45.0 all-gather.2
  63.5 101.8 all-gather.4

commit v7 on v6

--- a/solution.py
+++ b/solution.py
@@ -127,6 +127,11 @@
 
     _, out = lax.fori_loop(0, nb, body, (rhs, jnp.zeros((n, cols), jnp.float32)))
     return out
+
+
+def chunked_permute(x, axis, perm, parts=4):
+    pieces = jnp.split(x, parts, axis=0)
+    return jnp.concatenate([lax.ppermute(p, axis, perm) for p in pieces], axis=0)
 
 
 def on_device(front, anc_weight, solved, owners, indices, counts, rhs_side):
@@ -156,10 +161,8 @@
     w_rows = anc_weight.shape[0]
     fold = shard_rows // w_rows
     both = jnp.concatenate([front, anc_weight.reshape(shard_rows, width // fold)], axis=1)
-    for axis in ("xh", "z", "y"):
+    for axis in ("xh", "y", "z"):
         both = lax.all_gather(both, axis, axis=0, tiled=True)
-    n_y, n_z = lax.axis_size("y"), lax.axis_size("z")
-    both = both.reshape(n_y, n_z, -1, both.shape[1]).transpose(1, 0, 2, 3).reshape(-1, both.shape[1])
     front_tile = both
     weight_tile = both[:, width:].reshape(-1, w_rows, fold, width // fold).reshape(-1, width)
     anc_total = lax.dot_general(
@@ -175,7 +178,7 @@
     other_one = lax.ppermute(own_one, "row", [(0, 1)])
     reduced_one = rhs_values - own_one.astype(jnp.float32) - other_one.astype(jnp.float32)
     sol_one = kernel_solve(front_tile, prod, inv_diag, reduced_one)
-    got_one = lax.ppermute(sol_one, "col", left)
+    got_one = chunked_permute(sol_one, "col", left)
     sol_one = jnp.where(col_index == 1, sol_one, got_one)
 
     front_term = lax.dot_general(
@@ -186,7 +189,7 @@
     other_zero = lax.ppermute(own_zero, "row", down)
     reduced_zero = rhs_values - own_zero.astype(jnp.float32) - other_zero.astype(jnp.float32)
     sol_zero = kernel_solve(front_tile, prod, inv_diag, reduced_zero)
-    got_zero = lax.ppermute(sol_zero, "col", right)
+    got_zero = chunked_permute(sol_zero, "col", right)
     sol_zero = jnp.where(col_index == 0, sol_zero, got_zero)
     return jnp.where(row_index == 1, sol_one, sol_zero)
 

time: 283 us -> 271 us (0.958)
  local copies, waits for them, and re-layouts: 24.5 us -> 11.9 us
  starting transfers between devices: 12.1 us -> 21.5 us
  waiting for transfers between devices: 164 us -> 157 us
    ppermute x2 -> x8, starting transfers between devices: 5 us -> 14.4 us  [chunked_permute(): lax.ppermute(p, axis, perm)]
    ppermute x2 -> x8, waiting for transfers between devices: 25.3 us -> 16.2 us  [chunked_permute(): lax.ppermute(p, axis, perm)]
    reshape x1 -> x0, local copies, waits for them, and re-layouts: 9.05 us -> none  [on_device(): both.reshape(n_y, n_z, -1, both.shape[1]).transpose(1, 0, 2, 3)]
  transfers between devices with their start and end apart: 7 -> 13, of which waited for: 5 -> 12; matrix products, arithmetic and copies ran while one was open for 4% -> 2% of each run, Pallas kernels for 0% -> 0%
where the time goes in v7:
time: 271 us
  waiting for transfers between devices  157 us (58%)
  Pallas kernels  29.7 us (11%)
  matrix products  23.6 us (9%)
  starting transfers between devices  21.5 us (8%)
  between operations  13.9 us (5%)
  local copies, waits for them, and re-layouts  11.9 us (4%)
  blocking collectives  8.21 us (3%)
  other arithmetic  4.69 us (2%)
    all_gather x2, waiting for transfers between devices, on_device(): both = lax.all_gather(both, axis, axis=0, tiled=True)  136 us
    pallas_call x2, Pallas kernels, kernel_solve(): pl.pallas_call(solve_kernel, out_shape=jax.ShapeDtypeStruct((cols, n), jn...  27.7 us
    ppermute x8, waiting for transfers between devices, chunked_permute(): lax.ppermute(p, axis, perm)  16.2 us
    ppermute x8, starting transfers between devices, chunked_permute(): lax.ppermute(p, axis, perm)  14.4 us
    all_gather x1, blocking collectives, on_device(): both = lax.all_gather(both, axis, axis=0, tiled=True)  8.21 us
    dot_general x12, matrix products, mm3(): out = jnp.einsum(eq, a_hi, b_hi, preferred_element_type=jnp.float32)  5.52 us
  transfers between devices with their start and end apart: 13, of which 12 were waited for; matrix products, arithmetic and copies ran while one was open for 2% of the time, Pallas kernels for 0%

profile of v7, /device:TPU:6, one launch (start us, length us, event | category | flops | bytes accessed | tf_op | source)
XLA Modules:
  0.0 270.7 jit_solution(16000897187802480855)
XLA Ops:
  6.6 0.8 reshape.122
  7.4 1.0 pad_maximum_fusion
  8.4 8.2 %all_gather.9 = bf16[64,2560]{1,0:T(8,128)(2,1)} all-gather(bf16[32,2560]{1,0:T(8,128)(2,1)S(1)} %pad_maximum_fusion), channel_id=1, replica_groups=mesh['row'=2,'col'=2,'z'=8,'y'=4,'xh'=2] {'xh'}, dimensions={0}, use_global_device_ids=true | all-gather | bytes 491520 | tf_op jit(solution)/shard_map/all_gather | solution.py:165
  16.7 30.4 %all-gather.3.cloned.1.call-done = bf16[256,2560]{1,0:T(8,128)(2,1)} async-done(((bf16[64,2560]{1,0:T(8,128)(2,1)}), bf16[256,2560]{1,0:T(8,128)(2,1)}) %all-gather.3.cloned.1.call-update) | async-done | bytes 1310736 | tf_op jit(solution)/shard_map/all_gather | solution.py:165
  47.3 0.6 gather_fusion.1
  47.9 0.6 gather_fusion
  48.6 0.9 gather_fusion.2
  49.6 0.7 broadcast_in_dim.28
  50.3 4.1 %all-to-all-start = ((bf16[4,128,128]{2,1,0:T(8,128)(2,1)}), bf16[4,128,128]{2,1,0:T(8,128)(2,1)S(1)}, u32[]{:S(2)}, u32[]{:S(2)}) async-start(bf16[4,128,128]{2,1,0:T(8,128)(2,1)} %bitcast.5), calls=%async_computation | async-start | bytes 262144 | tf_op jit(solution)/shard_map/all_to_all | solution.py:157
  54.4 1.0 copy.13
  55.6 1.6 all-to-all-done
  57.2 0.6 gather_fusion.3
  57.8 105.4 %all-gather.5.cloned.1.call-done.t_hbm.f_ref = bf16[2048,2560]{1,0:T(8,128)(2,1)} async-done(((bf16[256,2560]{1,0:T(8,128)(2,1)}), bf16[2048,2560]{1,0:T(8,128)(2,1)}) %all-gather.5.cloned.1.call-update) | async-done | bytes 10485776 | tf_op jit(solution)/shard_map/all_gather | solution.py:165
  163.2 2.0 shard_map.73
  165.2 1.4 fusion.12
  166.6 2.1 fusion.27
  168.6 0.9 convolution_add_fusion.23
  169.5 0.9 convolution_add_fusion.22
  180.4 0.7 copy-done.2
  181.1 1.3 convolution_add_fusion.1
  182.4 1.6 slice-done
  184.0 2.6 reshape_reshape.3
  186.6 3.2 %fusion.83 = (bf16[2048,128]{0,1:T(8,128)(2,1)S(1)}, f32[2048,128]{0,1:T(8,128)}) fusion(bf16[512,2048]{1,0:T(8,128)(2,1)} %reshape_reshape.3, bf16[512,128]{1,0:T(8,128)(2,1)S(1)} %bitcast.26), kind=kOutput, calls=%fused_computation.145 | convolution fusion | flops 268697600 | bytes 3801088 | tf_op jit(solution)/shard_map/dot_general | solution.py:168
  189.8 1.6 collective-permute-start
  191.8 1.1 collective-permute-done
  193.2 13.9 %shard_map.74 = bf16[128,2048]{1,0:T(8,128)(2,1)S(1)} custom-call(bf16[2048,2560]{1,0:T(8,128)(2,1)} %all-gather.5.cloned.1.call-done.t_hbm.f_ref, f32[16,128,128]{2,1,0:T(8,128)S(1)} %convolution_add_fusion.p_ref, f32[16,128]{1,0:T(8,128)S(1)} %broadcast_divide_fusion.d_ref, f32[128,2048]{1,0:T(8,128)S(1)} %fusion.15.r_ref), custom_call_target="tpu_custom_call" | custom-call | tf_op jit(solution)/shard_map/pallas_call | solution.py:100
  207.1 0.7 fusion.82
  207.8 3.4 %collective-permute-start.1 = (bf16[512,128]{0,1:T(8,128)(2,1)}, bf16[512,128]{0,1:T(8,128)(2,1)}, u32[]{:S(2)}, u32[]{:S(2)}) collective-permute-start(bf16[512,128]{0,1:T(8,128)(2,1)} %get-tuple-element.9), channel_id=1, source_target_pairs={{64,0},{65,1},{66,2},{67,3},{68,4},{69,5},{70,6},{71,7},{72,8},{73... | collective-permute-start | bytes 393224 | tf_op jit(solution)/shard_map/ppermute | solution.py:134
  211.2 1.9 collective-permute-start.2
  213.2 1.9 collective-permute-start.3
  215.1 1.9 collective-permute-start.4
  217.1 0.5 collective-permute-done.2
  217.6 2.7 collective-permute-done.3
  220.3 2.2 collective-permute-done.4
  222.5 5.1 %fusion.8 = bf16[2048,128]{0,1:T(8,128)(2,1)S(1)} fusion(bf16[2048,128]{0,1:T(8,128)(2,1)S(1)} %copy-done.7, f32[2048,128]{0,1:T(8,128)S(1)} %copy-done.9, bf16[2048,2560]{1,0:T(8,128)(2,1)} %all-gather.5.cloned.1.call-done.t_hbm.f_ref, pred[]{:T(512)S(6)} %eq.49, bf16[512,128]{0,1:T(8,128)(2,1)} %collective-permute-done.4, ...), kind=kOutput, calls=%fused_computation.8 | convolution fusion | flops 1076887552 | bytes 11534338 | tf_op jit(solution)/shard_map/dot_general | solution.py:184
  227.6 1.3 collective-permute-start.5
  228.9 2.5 collective-permute-done.5
  231.6 13.8 %shard_map.75 = bf16[128,2048]{1,0:T(8,128)(2,1)S(1)} custom-call(bf16[2048,2560]{1,0:T(8,128)(2,1)} %all-gather.5.cloned.1.call-done.t_hbm.f_ref, f32[16,128,128]{2,1,0:T(8,128)S(1)} %convolution_add_fusion.p_ref, f32[16,128]{1,0:T(8,128)S(1)} %broadcast_divide_fusion.d_ref, f32[128,2048]{1,0:T(8,128)S(1)} %fusion.17.r_ref), custom_call_target="tpu_custom_call" | custom-call | tf_op jit(solution)/shard_map/pallas_call | solution.py:100
  245.4 1.3 collective-permute-start.6
  246.7 1.3 collective-permute-start.7
  248.0 1.3 collective-permute-start.8
  249.3 1.3 collective-permute-start.9
  250.6 3.1 %collective-permute-done.6 = bf16[512,128]{0,1:T(8,128)(2,1)S(1)} collective-permute-done((bf16[512,128]{0,1:T(8,128)(2,1)S(1)}, bf16[512,128]{0,1:T(8,128)(2,1)S(1)}, u32[]{:S(2)}, u32[]{:S(2)}) %collective-permute-start.6) | collective-permute-done | bytes 131104 | tf_op jit(solution)/shard_map/ppermute | solution.py:134
  253.7 2.8 %collective-permute-done.7 = bf16[512,128]{0,1:T(8,128)(2,1)S(1)} collective-permute-done((bf16[512,128]{0,1:T(8,128)(2,1)S(1)}, bf16[512,128]{0,1:T(8,128)(2,1)S(1)}, u32[]{:S(2)}, u32[]{:S(2)}) %collective-permute-start.7) | collective-permute-done | bytes 131104 | tf_op jit(solution)/shard_map/ppermute | solution.py:134
  256.5 2.8 %collective-permute-done.8 = bf16[512,128]{0,1:T(8,128)(2,1)S(1)} collective-permute-done((bf16[512,128]{0,1:T(8,128)(2,1)S(1)}, bf16[512,128]{0,1:T(8,128)(2,1)S(1)}, u32[]{:S(2)}, u32[]{:S(2)}) %collective-permute-start.8) | collective-permute-done | bytes 131104 | tf_op jit(solution)/shard_map/ppermute | solution.py:134
  259.3 2.2 collective-permute-done.9
  261.5 1.4 fusion.18
  262.9 1.0 copy.17
  (82 shorter events, 11.4 us)
Async XLA Ops:
  6.5 42.0 %copy-start = (bf16[512,128]{1,0:T(8,128)(2,1)S(1)}, bf16[512,128]{1,0:T(8,128)(2,1)}, u32[]{:S(2)}) copy-start(bf16[512,128]{1,0:T(8,128)(2,1)} %param.9) | copy-start | bytes 393220
  6.5 40.5 %copy-start.13 = (s32[8]{0:T(128)S(1)}, s32[8]{0:T(128)}, u32[]{:S(2)}) copy-start(s32[8]{0:T(128)} %param.10) | copy-start | bytes 100
  6.5 40.8 %copy-start.12 = (s32[8,128]{1,0:T(8,128)S(1)}, s32[8,128]{1,0:T(8,128)}, u32[]{:S(2)}) copy-start(s32[8,128]{1,0:T(8,128)} %param.11) | copy-start | bytes 12292
  6.5 41.4 %copy-start.1 = (s32[8]{0:T(128)S(1)}, s32[8]{0:T(128)}, u32[]{:S(2)}) copy-start(s32[8]{0:T(128)} %param.12) | copy-start | bytes 100
  6.5 40.5 %all-gather.3.cloned.1.call-start = ((), (), s32[]{:S(2)}) async-start(), calls=%async_computation.1 | async-start | bytes 1638400 | tf_op jit(solution)/shard_map/all_gather | solution.py:165
  7.4 47.0 %copy-start.11 = (bf16[2048,128]{1,0:T(8,128)(2,1)S(1)}, bf16[2048,128]{1,0:T(8,128)(2,1)}, u32[]{:S(2)}) copy-start(bf16[2048,128]{1,0:T(8,128)(2,1)} %param.13) | copy-start | bytes 1572868
  16.6 146.5 %all-gather.5.cloned.1.call-start = ((), (), s32[]{:S(2)}) async-start(), calls=%async_computation.2 | async-start | bytes 11796480 | tf_op jit(solution)/shard_map/all_gather | solution.py:165
  50.3 6.9 %all-to-all-start = ((bf16[4,128,128]{2,1,0:T(8,128)(2,1)}), bf16[4,128,128]{2,1,0:T(8,128)(2,1)S(1)}, u32[]{:S(2)}, u32[]{:S(2)}) async-start(bf16[4,128,128]{2,1,0:T(8,128)(2,1)} %bitcast.5), calls=%async_computation | async-start | bytes 262144 | tf_op jit(solution)/shard_map/all_to_all | solution.py:157
  166.5 2.1 copy-start.10
  180.1 1.0 copy-start.2
  182.4 1.6 slice-start
  186.6 4.8 %copy-start.3 = (f32[16,128,128]{2,1,0:T(8,128)S(1)}, f32[16,128,128]{2,1,0:T(8,128)}, u32[]{:S(2)}) copy-start(f32[16,128,128]{2,1,0:T(8,128)} %copy-done.2) | copy-start | bytes 3145732
  186.6 4.9 %copy-start.8 = (f32[16,128,128]{2,1,0:T(8,128)S(1)}, f32[16,128,128]{2,1,0:T(8,128)}, u32[]{:S(2)}) copy-start(f32[16,128,128]{2,1,0:T(8,128)} %convolution_add_fusion.1) | copy-start | bytes 3145732
  189.8 3.1 %copy-start.6 = (bf16[2048,128]{0,1:T(8,128)(2,1)}, bf16[2048,128]{0,1:T(8,128)(2,1)S(1)}, u32[]{:S(2)}) copy-start(bf16[2048,128]{0,1:T(8,128)(2,1)S(1)} %get-tuple-element.13) | copy-start | bytes 1572868
  189.8 3.1 %collective-permute-start = (bf16[2048,128]{0,1:T(8,128)(2,1)S(1)}, bf16[2048,128]{0,1:T(8,128)(2,1)S(1)}, u32[]{:S(2)}, u32[]{:S(2)}) collective-permute-start(bf16[2048,128]{0,1:T(8,128)(2,1)S(1)} %get-tuple-element.13), channel_id=1, source_target_pairs={{0,128},{1,129},{2,130},{3,131},{4,132},{5,133},{6,134},{7,135},{8... | collective-permute-start | bytes 1572872 | tf_op jit(solution)/shard_map/ppermute | solution.py:178
  191.5 1.5 copy-start.4
  193.2 29.3 %copy-start.7 = (bf16[2048,128]{0,1:T(8,128)(2,1)S(1)}, bf16[2048,128]{0,1:T(8,128)(2,1)}, u32[]{:S(2)}) copy-start(bf16[2048,128]{0,1:T(8,128)(2,1)} %copy-done.6) | copy-start | bytes 1572868
  193.2 29.3 %copy-start.9 = (f32[2048,128]{0,1:T(8,128)S(1)}, f32[2048,128]{0,1:T(8,128)}, u32[]{:S(2)}) copy-start(f32[2048,128]{0,1:T(8,128)} %get-tuple-element.14) | copy-start | bytes 3145732
  207.8 9.2 %collective-permute-start.1 = (bf16[512,128]{0,1:T(8,128)(2,1)}, bf16[512,128]{0,1:T(8,128)(2,1)}, u32[]{:S(2)}, u32[]{:S(2)}) collective-permute-start(bf16[512,128]{0,1:T(8,128)(2,1)} %get-tuple-element.9), channel_id=1, source_target_pairs={{64,0},{65,1},{66,2},{67,3},{68,4},{69,5},{70,6},{71,7},{72,8},{73... | collective-permute-start | bytes 393224 | tf_op jit(solution)/shard_map/ppermute | solution.py:134
  211.2 6.4 %collective-permute-start.2 = (bf16[512,128]{0,1:T(8,128)(2,1)}, bf16[512,128]{0,1:T(8,128)(2,1)}, u32[]{:S(2)}, u32[]{:S(2)}) collective-permute-start(bf16[512,128]{0,1:T(8,128)(2,1)} %get-tuple-element.12), channel_id=1, source_target_pairs={{64,0},{65,1},{66,2},{67,3},{68,4},{69,5},{70,6},{71,7},{72,8},{73... | collective-permute-start | bytes 393224 | tf_op jit(solution)/shard_map/ppermute | solution.py:134
  213.2 7.1 %collective-permute-start.3 = (bf16[512,128]{0,1:T(8,128)(2,1)S(1)}, bf16[512,128]{0,1:T(8,128)(2,1)}, u32[]{:S(2)}, u32[]{:S(2)}) collective-permute-start(bf16[512,128]{0,1:T(8,128)(2,1)S(1)} %get-tuple-element.11), channel_id=1, source_target_pairs={{64,0},{65,1},{66,2},{67,3},{68,4},{69,5},{70,6},{71,7},{72,8},{73... | collective-permute-start | bytes 393224 | tf_op jit(solution)/shard_map/ppermute | solution.py:134
  215.1 7.3 %collective-permute-start.4 = (bf16[512,128]{0,1:T(8,128)(2,1)S(1)}, bf16[512,128]{0,1:T(8,128)(2,1)}, u32[]{:S(2)}, u32[]{:S(2)}) collective-permute-start(bf16[512,128]{0,1:T(8,128)(2,1)S(1)} %get-tuple-element.10), channel_id=1, source_target_pairs={{64,0},{65,1},{66,2},{67,3},{68,4},{69,5},{70,6},{71,7},{72,8},{73... | collective-permute-start | bytes 393224 | tf_op jit(solution)/shard_map/ppermute | solution.py:134
  222.5 8.9 %copy-start.5 = (bf16[2048,128]{0,1:T(8,128)(2,1)S(1)}, bf16[2048,128]{0,1:T(8,128)(2,1)}, u32[]{:S(2)}) copy-start(bf16[2048,128]{0,1:T(8,128)(2,1)} %copy.13) | copy-start | bytes 1572868
  227.6 3.8 %collective-permute-start.5 = (bf16[2048,128]{0,1:T(8,128)(2,1)S(1)}, bf16[2048,128]{0,1:T(8,128)(2,1)S(1)}, u32[]{:S(2)}, u32[]{:S(2)}) collective-permute-start(bf16[2048,128]{0,1:T(8,128)(2,1)S(1)} %fusion.8), channel_id=1, source_target_pairs={{128,0},{129,1},{130,2},{131,3},{132,4},{133,5},{134,6},{135,7},{1... | collective-permute-start | bytes 1572872 | tf_op jit(solution)/shard_map/ppermute | solution.py:189
  245.4 8.3 %collective-permute-start.6 = (bf16[512,128]{0,1:T(8,128)(2,1)S(1)}, bf16[512,128]{0,1:T(8,128)(2,1)S(1)}, u32[]{:S(2)}, u32[]{:S(2)}) collective-permute-start(bf16[512,128]{0,1:T(8,128)(2,1)S(1)} %get-tuple-element.5), channel_id=1, source_target_pairs={{0,64},{1,65},{2,66},{3,67},{4,68},{5,69},{6,70},{7,71},{8,72},{9,... | collective-permute-start | bytes 393224 | tf_op jit(solution)/shard_map/ppermute | solution.py:134
  246.7 9.8 %collective-permute-start.7 = (bf16[512,128]{0,1:T(8,128)(2,1)S(1)}, bf16[512,128]{0,1:T(8,128)(2,1)S(1)}, u32[]{:S(2)}, u32[]{:S(2)}) collective-permute-start(bf16[512,128]{0,1:T(8,128)(2,1)S(1)} %get-tuple-element.8), channel_id=1, source_target_pairs={{0,64},{1,65},{2,66},{3,67},{4,68},{5,69},{6,70},{7,71},{8,72},{9,... | collective-permute-start | bytes 393224 | tf_op jit(solution)/shard_map/ppermute | solution.py:134
  248.0 11.3 %collective-permute-start.8 = (bf16[512,128]{0,1:T(8,128)(2,1)S(1)}, bf16[512,128]{0,1:T(8,128)(2,1)S(1)}, u32[]{:S(2)}, u32[]{:S(2)}) collective-permute-start(bf16[512,128]{0,1:T(8,128)(2,1)S(1)} %get-tuple-element.7), channel_id=1, source_target_pairs={{0,64},{1,65},{2,66},{3,67},{4,68},{5,69},{6,70},{7,71},{8,72},{9,... | collective-permute-start | bytes 393224 | tf_op jit(solution)/shard_map/ppermute | solution.py:134
  249.3 12.1 %collective-permute-start.9 = (bf16[512,128]{0,1:T(8,128)(2,1)S(1)}, bf16[512,128]{0,1:T(8,128)(2,1)S(1)}, u32[]{:S(2)}, u32[]{:S(2)}) collective-permute-start(bf16[512,128]{0,1:T(8,128)(2,1)S(1)} %get-tuple-element.6), channel_id=1, source_target_pairs={{0,64},{1,65},{2,66},{3,67},{4,68},{5,69},{6,70},{7,71},{8,72},{9,... | collective-permute-start | bytes 393224 | tf_op jit(solution)/shard_map/ppermute | solution.py:134
Sparse Core Ops, SparseCore 0:
  16.8 30.2 all-gather.2
  48.8 114.2 all-gather.4

commit v8 on v7

--- a/solution.py
+++ b/solution.py
@@ -6,15 +6,6 @@
 from jax.experimental.pallas import tpu as pltpu
 
 BLOCK = 128
-HIGH = lax.Precision.HIGHEST
-
-
-def split_dot_t(mat_bf16, vec_f32):
-    hi = vec_f32.astype(jnp.bfloat16)
-    lo = (vec_f32 - hi.astype(jnp.float32)).astype(jnp.bfloat16)
-    dims = (((0,), (0,)), ((), ()))
-    out = lax.dot_general(mat_bf16, hi, dims, preferred_element_type=jnp.float32)
-    return out + lax.dot_general(mat_bf16, lo, dims, preferred_element_type=jnp.float32)
 
 
 def split_bf16(x):
@@ -108,33 +99,12 @@
     return out_t.T
 
 
-def apply_solve(tile, prod, inv_diag, rhs):
-    n = tile.shape[0]
-    nb = n // BLOCK
-    cols = rhs.shape[1]
-
-    def body(i, carry):
-        rest, out = carry
-        j = nb - 1 - i
-        r_j = lax.dynamic_slice_in_dim(rest, j * BLOCK, BLOCK, 0)
-        p_j = lax.dynamic_index_in_dim(prod, j, 0, keepdims=False)
-        d_j = lax.dynamic_index_in_dim(inv_diag, j, 0, keepdims=False)
-        v_j = jnp.einsum("ji,jk->ik", p_j, r_j, precision=HIGH) * d_j[:, None]
-        rows = lax.dynamic_slice_in_dim(tile, j * BLOCK, BLOCK, 0)
-        rest = rest - split_dot_t(rows, v_j)
-        out = lax.dynamic_update_slice_in_dim(out, v_j, j * BLOCK, 0)
-        return rest, out
-
-    _, out = lax.fori_loop(0, nb, body, (rhs, jnp.zeros((n, cols), jnp.float32)))
-    return out
-
-
 def chunked_permute(x, axis, perm, parts=4):
     pieces = jnp.split(x, parts, axis=0)
     return jnp.concatenate([lax.ppermute(p, axis, perm) for p in pieces], axis=0)
 
 
-def on_device(front, anc_weight, solved, owners, indices, counts, rhs_side):
+def ancestor_values(solved, owners, indices, counts):
     row_count = lax.axis_size("row")
     col_count = lax.axis_size("col")
     tiles_block = row_count * col_count
@@ -157,12 +127,20 @@
     received = lax.all_to_all(outgoing, ("row", "col"), split_axis=0, concat_axis=0, tiled=True)
     slot_rows = received.reshape(tiles_block, tile_rows, columns)
     anc_values = slot_rows[block_owners].reshape(tiles_block * tile_rows, columns)
+    return anc_values
+
+
+def device_body(front, anc_weight, solved, owners, indices, counts, rhs_side):
+    row_index = lax.axis_index("row")
+    col_index = lax.axis_index("col")
     shard_rows, width = front.shape
     w_rows = anc_weight.shape[0]
     fold = shard_rows // w_rows
     both = jnp.concatenate([front, anc_weight.reshape(shard_rows, width // fold)], axis=1)
-    for axis in ("xh", "y", "z"):
-        both = lax.all_gather(both, axis, axis=0, tiled=True)
+    both = lax.all_gather(both, "xh", axis=0, tiled=True)
+    both = lax.all_gather(both, "y", axis=0, tiled=True)
+    anc_values = ancestor_values(solved, owners, indices, counts)
+    both = lax.all_gather(both, "z", axis=0, tiled=True)
     front_tile = both
     weight_tile = both[:, width:].reshape(-1, w_rows, fold, width // fold).reshape(-1, width)
     anc_total = lax.dot_general(
@@ -211,5 +189,5 @@
         P("row", rhs),
     )
     return jax.shard_map(
-        on_device, mesh=sub, in_specs=placed, out_specs=P("row", rhs), check_vma=False
+        device_body, mesh=sub, in_specs=placed, out_specs=P("row", rhs), check_vma=False
     )

time: 271 us -> 271 us (level)
  no operation moved by 1% of the time
where the time goes in v8:
time: 271 us
  waiting for transfers between devices  157 us (58%)
  Pallas kernels  29.7 us (11%)
  matrix products  23.6 us (9%)
  starting transfers between devices  21.5 us (8%)
  between operations  13.9 us (5%)
  local copies, waits for them, and re-layouts  11.9 us (4%)
  blocking collectives  8.21 us (3%)
  other arithmetic  4.69 us (2%)
    all_gather x1, waiting for transfers between devices, device_body(): both = lax.all_gather(both, 'z', axis=0, tiled=True)  105 us
    all_gather x1, waiting for transfers between devices, device_body(): both = lax.all_gather(both, 'y', axis=0, tiled=True)  30.4 us
    pallas_call x2, Pallas kernels, kernel_solve(): pl.pallas_call(solve_kernel, out_shape=jax.ShapeDtypeStruct((cols, n), jn...  27.7 us
    ppermute x8, waiting for transfers between devices, chunked_permute(): lax.ppermute(p, axis, perm)  16.2 us
    ppermute x8, starting transfers between devices, chunked_permute(): lax.ppermute(p, axis, perm)  14.4 us
    all_gather x1, blocking collectives, device_body(): both = lax.all_gather(both, 'xh', axis=0, tiled=True)  8.21 us
    dot_general x12, matrix products, mm3(): out = jnp.einsum(eq, a_hi, b_hi, preferred_element_type=jnp.float32)  5.52 us
  transfers between devices with their start and end apart: 13, of which 12 were waited for; matrix products, arithmetic and copies ran while one was open for 2% of the time, Pallas kernels for 0%

profile of v8, /device:TPU:6, one launch (start us, length us, event | category | flops | bytes accessed | tf_op | source)
XLA Modules:
  0.0 270.7 jit_solution(16000897187802480855)
XLA Ops:
  6.6 0.8 reshape.122
  7.4 1.0 pad_maximum_fusion
  8.4 8.2 %all_gather.9 = bf16[64,2560]{1,0:T(8,128)(2,1)} all-gather(bf16[32,2560]{1,0:T(8,128)(2,1)S(1)} %pad_maximum_fusion), channel_id=1, replica_groups=mesh['row'=2,'col'=2,'z'=8,'y'=4,'xh'=2] {'xh'}, dimensions={0}, use_global_device_ids=true | all-gather | bytes 491520 | tf_op jit(solution)/shard_map/all_gather | solution.py:140
  16.7 30.4 %all-gather.3.cloned.1.call-done = bf16[256,2560]{1,0:T(8,128)(2,1)} async-done(((bf16[64,2560]{1,0:T(8,128)(2,1)}), bf16[256,2560]{1,0:T(8,128)(2,1)}) %all-gather.3.cloned.1.call-update) | async-done | bytes 1310736 | tf_op jit(solution)/shard_map/all_gather | solution.py:141
  47.3 0.6 gather_fusion.1
  47.9 0.6 gather_fusion
  48.6 0.9 gather_fusion.2
  49.6 0.7 broadcast_in_dim.28
  50.3 4.1 %all-to-all-start = ((bf16[4,128,128]{2,1,0:T(8,128)(2,1)}), bf16[4,128,128]{2,1,0:T(8,128)(2,1)S(1)}, u32[]{:S(2)}, u32[]{:S(2)}) async-start(bf16[4,128,128]{2,1,0:T(8,128)(2,1)} %bitcast.5), calls=%async_computation | async-start | bytes 262144 | tf_op jit(solution)/shard_map/all_to_all | solution.py:127
  54.4 1.0 copy.13
  55.6 1.6 all-to-all-done
  57.2 0.6 gather_fusion.3
  57.8 105.4 %all-gather.5.cloned.1.call-done.t_hbm.f_ref = bf16[2048,2560]{1,0:T(8,128)(2,1)} async-done(((bf16[256,2560]{1,0:T(8,128)(2,1)}), bf16[2048,2560]{1,0:T(8,128)(2,1)}) %all-gather.5.cloned.1.call-update) | async-done | bytes 10485776 | tf_op jit(solution)/shard_map/all_gather | solution.py:143
  163.2 2.0 shard_map.73
  165.2 1.4 fusion.12
  166.6 2.1 fusion.27
  168.6 0.9 convolution_add_fusion.23
  169.5 0.9 convolution_add_fusion.22
  180.4 0.7 copy-done.2
  181.1 1.3 convolution_add_fusion.1
  182.4 1.6 slice-done
  184.0 2.6 reshape_reshape.3
  186.6 3.2 %fusion.83 = (bf16[2048,128]{0,1:T(8,128)(2,1)S(1)}, f32[2048,128]{0,1:T(8,128)}) fusion(bf16[512,2048]{1,0:T(8,128)(2,1)} %reshape_reshape.3, bf16[512,128]{1,0:T(8,128)(2,1)S(1)} %bitcast.26), kind=kOutput, calls=%fused_computation.145 | convolution fusion | flops 268697600 | bytes 3801088 | tf_op jit(solution)/shard_map/dot_general | solution.py:146
  189.8 1.6 collective-permute-start
  191.8 1.1 collective-permute-done
  193.2 13.9 %shard_map.74 = bf16[128,2048]{1,0:T(8,128)(2,1)S(1)} custom-call(bf16[2048,2560]{1,0:T(8,128)(2,1)} %all-gather.5.cloned.1.call-done.t_hbm.f_ref, f32[16,128,128]{2,1,0:T(8,128)S(1)} %convolution_add_fusion.p_ref, f32[16,128]{1,0:T(8,128)S(1)} %broadcast_divide_fusion.d_ref, f32[128,2048]{1,0:T(8,128)S(1)} %fusion.15.r_ref), custom_call_target="tpu_custom_call" | custom-call | tf_op jit(solution)/shard_map/pallas_call | solution.py:91
  207.1 0.7 fusion.82
  207.8 3.4 %collective-permute-start.1 = (bf16[512,128]{0,1:T(8,128)(2,1)}, bf16[512,128]{0,1:T(8,128)(2,1)}, u32[]{:S(2)}, u32[]{:S(2)}) collective-permute-start(bf16[512,128]{0,1:T(8,128)(2,1)} %get-tuple-element.9), channel_id=1, source_target_pairs={{64,0},{65,1},{66,2},{67,3},{68,4},{69,5},{70,6},{71,7},{72,8},{73... | collective-permute-start | bytes 393224 | tf_op jit(solution)/shard_map/ppermute | solution.py:104
  211.2 1.9 collective-permute-start.2
  213.2 1.9 collective-permute-start.3
  215.1 1.9 collective-permute-start.4
  217.1 0.5 collective-permute-done.2
  217.6 2.7 collective-permute-done.3
  220.3 2.2 collective-permute-done.4
  222.5 5.1 %fusion.8 = bf16[2048,128]{0,1:T(8,128)(2,1)S(1)} fusion(bf16[2048,128]{0,1:T(8,128)(2,1)S(1)} %copy-done.7, f32[2048,128]{0,1:T(8,128)S(1)} %copy-done.9, bf16[2048,2560]{1,0:T(8,128)(2,1)} %all-gather.5.cloned.1.call-done.t_hbm.f_ref, pred[]{:T(512)S(6)} %eq.49, bf16[512,128]{0,1:T(8,128)(2,1)} %collective-permute-done.4, ...), kind=kOutput, calls=%fused_computation.8 | convolution fusion | flops 1076887552 | bytes 11534338 | tf_op jit(solution)/shard_map/dot_general | solution.py:162
  227.6 1.3 collective-permute-start.5
  228.9 2.5 collective-permute-done.5
  231.6 13.8 %shard_map.75 = bf16[128,2048]{1,0:T(8,128)(2,1)S(1)} custom-call(bf16[2048,2560]{1,0:T(8,128)(2,1)} %all-gather.5.cloned.1.call-done.t_hbm.f_ref, f32[16,128,128]{2,1,0:T(8,128)S(1)} %convolution_add_fusion.p_ref, f32[16,128]{1,0:T(8,128)S(1)} %broadcast_divide_fusion.d_ref, f32[128,2048]{1,0:T(8,128)S(1)} %fusion.17.r_ref), custom_call_target="tpu_custom_call" | custom-call | tf_op jit(solution)/shard_map/pallas_call | solution.py:91
  245.4 1.3 collective-permute-start.6
  246.7 1.3 collective-permute-start.7
  248.0 1.3 collective-permute-start.8
  249.3 1.3 collective-permute-start.9
  250.6 3.1 %collective-permute-done.6 = bf16[512,128]{0,1:T(8,128)(2,1)S(1)} collective-permute-done((bf16[512,128]{0,1:T(8,128)(2,1)S(1)}, bf16[512,128]{0,1:T(8,128)(2,1)S(1)}, u32[]{:S(2)}, u32[]{:S(2)}) %collective-permute-start.6) | collective-permute-done | bytes 131104 | tf_op jit(solution)/shard_map/ppermute | solution.py:104
  253.7 2.8 %collective-permute-done.7 = bf16[512,128]{0,1:T(8,128)(2,1)S(1)} collective-permute-done((bf16[512,128]{0,1:T(8,128)(2,1)S(1)}, bf16[512,128]{0,1:T(8,128)(2,1)S(1)}, u32[]{:S(2)}, u32[]{:S(2)}) %collective-permute-start.7) | collective-permute-done | bytes 131104 | tf_op jit(solution)/shard_map/ppermute | solution.py:104
  256.5 2.8 %collective-permute-done.8 = bf16[512,128]{0,1:T(8,128)(2,1)S(1)} collective-permute-done((bf16[512,128]{0,1:T(8,128)(2,1)S(1)}, bf16[512,128]{0,1:T(8,128)(2,1)S(1)}, u32[]{:S(2)}, u32[]{:S(2)}) %collective-permute-start.8) | collective-permute-done | bytes 131104 | tf_op jit(solution)/shard_map/ppermute | solution.py:104
  259.3 2.2 collective-permute-done.9
  261.5 1.4 fusion.18
  262.9 1.0 copy.17
  (82 shorter events, 11.4 us)
Async XLA Ops:
  6.5 42.0 %copy-start = (bf16[512,128]{1,0:T(8,128)(2,1)S(1)}, bf16[512,128]{1,0:T(8,128)(2,1)}, u32[]{:S(2)}) copy-start(bf16[512,128]{1,0:T(8,128)(2,1)} %param.9) | copy-start | bytes 393220
  6.5 40.5 %copy-start.13 = (s32[8]{0:T(128)S(1)}, s32[8]{0:T(128)}, u32[]{:S(2)}) copy-start(s32[8]{0:T(128)} %param.10) | copy-start | bytes 100
  6.5 40.8 %copy-start.12 = (s32[8,128]{1,0:T(8,128)S(1)}, s32[8,128]{1,0:T(8,128)}, u32[]{:S(2)}) copy-start(s32[8,128]{1,0:T(8,128)} %param.11) | copy-start | bytes 12292
  6.5 41.4 %copy-start.1 = (s32[8]{0:T(128)S(1)}, s32[8]{0:T(128)}, u32[]{:S(2)}) copy-start(s32[8]{0:T(128)} %param.12) | copy-start | bytes 100
  6.5 40.5 %all-gather.3.cloned.1.call-start = ((), (), s32[]{:S(2)}) async-start(), calls=%async_computation.1 | async-start | bytes 1638400 | tf_op jit(solution)/shard_map/all_gather | solution.py:141
  7.4 47.0 %copy-start.11 = (bf16[2048,128]{1,0:T(8,128)(2,1)S(1)}, bf16[2048,128]{1,0:T(8,128)(2,1)}, u32[]{:S(2)}) copy-start(bf16[2048,128]{1,0:T(8,128)(2,1)} %param.13) | copy-start | bytes 1572868
  16.6 146.5 %all-gather.5.cloned.1.call-start = ((), (), s32[]{:S(2)}) async-start(), calls=%async_computation.2 | async-start | bytes 11796480 | tf_op jit(solution)/shard_map/all_gather | solution.py:143
  50.3 6.9 %all-to-all-start = ((bf16[4,128,128]{2,1,0:T(8,128)(2,1)}), bf16[4,128,128]{2,1,0:T(8,128)(2,1)S(1)}, u32[]{:S(2)}, u32[]{:S(2)}) async-start(bf16[4,128,128]{2,1,0:T(8,128)(2,1)} %bitcast.5), calls=%async_computation | async-start | bytes 262144 | tf_op jit(solution)/shard_map/all_to_all | solution.py:127
  166.5 2.1 copy-start.10
  180.1 1.0 copy-start.2
  182.4 1.6 slice-start
  186.6 4.8 %copy-start.3 = (f32[16,128,128]{2,1,0:T(8,128)S(1)}, f32[16,128,128]{2,1,0:T(8,128)}, u32[]{:S(2)}) copy-start(f32[16,128,128]{2,1,0:T(8,128)} %copy-done.2) | copy-start | bytes 3145732
  186.6 4.9 %copy-start.8 = (f32[16,128,128]{2,1,0:T(8,128)S(1)}, f32[16,128,128]{2,1,0:T(8,128)}, u32[]{:S(2)}) copy-start(f32[16,128,128]{2,1,0:T(8,128)} %convolution_add_fusion.1) | copy-start | bytes 3145732
  189.8 3.1 %copy-start.6 = (bf16[2048,128]{0,1:T(8,128)(2,1)}, bf16[2048,128]{0,1:T(8,128)(2,1)S(1)}, u32[]{:S(2)}) copy-start(bf16[2048,128]{0,1:T(8,128)(2,1)S(1)} %get-tuple-element.13) | copy-start | bytes 1572868
  189.8 3.1 %collective-permute-start = (bf16[2048,128]{0,1:T(8,128)(2,1)S(1)}, bf16[2048,128]{0,1:T(8,128)(2,1)S(1)}, u32[]{:S(2)}, u32[]{:S(2)}) collective-permute-start(bf16[2048,128]{0,1:T(8,128)(2,1)S(1)} %get-tuple-element.13), channel_id=1, source_target_pairs={{0,128},{1,129},{2,130},{3,131},{4,132},{5,133},{6,134},{7,135},{8... | collective-permute-start | bytes 1572872 | tf_op jit(solution)/shard_map/ppermute | solution.py:156
  191.5 1.5 copy-start.4
  193.2 29.3 %copy-start.7 = (bf16[2048,128]{0,1:T(8,128)(2,1)S(1)}, bf16[2048,128]{0,1:T(8,128)(2,1)}, u32[]{:S(2)}) copy-start(bf16[2048,128]{0,1:T(8,128)(2,1)} %copy-done.6) | copy-start | bytes 1572868
  193.2 29.3 %copy-start.9 = (f32[2048,128]{0,1:T(8,128)S(1)}, f32[2048,128]{0,1:T(8,128)}, u32[]{:S(2)}) copy-start(f32[2048,128]{0,1:T(8,128)} %get-tuple-element.14) | copy-start | bytes 3145732
  207.8 9.2 %collective-permute-start.1 = (bf16[512,128]{0,1:T(8,128)(2,1)}, bf16[512,128]{0,1:T(8,128)(2,1)}, u32[]{:S(2)}, u32[]{:S(2)}) collective-permute-start(bf16[512,128]{0,1:T(8,128)(2,1)} %get-tuple-element.9), channel_id=1, source_target_pairs={{64,0},{65,1},{66,2},{67,3},{68,4},{69,5},{70,6},{71,7},{72,8},{73... | collective-permute-start | bytes 393224 | tf_op jit(solution)/shard_map/ppermute | solution.py:104
  211.2 6.4 %collective-permute-start.2 = (bf16[512,128]{0,1:T(8,128)(2,1)}, bf16[512,128]{0,1:T(8,128)(2,1)}, u32[]{:S(2)}, u32[]{:S(2)}) collective-permute-start(bf16[512,128]{0,1:T(8,128)(2,1)} %get-tuple-element.12), channel_id=1, source_target_pairs={{64,0},{65,1},{66,2},{67,3},{68,4},{69,5},{70,6},{71,7},{72,8},{73... | collective-permute-start | bytes 393224 | tf_op jit(solution)/shard_map/ppermute | solution.py:104
  213.2 7.1 %collective-permute-start.3 = (bf16[512,128]{0,1:T(8,128)(2,1)S(1)}, bf16[512,128]{0,1:T(8,128)(2,1)}, u32[]{:S(2)}, u32[]{:S(2)}) collective-permute-start(bf16[512,128]{0,1:T(8,128)(2,1)S(1)} %get-tuple-element.11), channel_id=1, source_target_pairs={{64,0},{65,1},{66,2},{67,3},{68,4},{69,5},{70,6},{71,7},{72,8},{73... | collective-permute-start | bytes 393224 | tf_op jit(solution)/shard_map/ppermute | solution.py:104
  215.1 7.3 %collective-permute-start.4 = (bf16[512,128]{0,1:T(8,128)(2,1)S(1)}, bf16[512,128]{0,1:T(8,128)(2,1)}, u32[]{:S(2)}, u32[]{:S(2)}) collective-permute-start(bf16[512,128]{0,1:T(8,128)(2,1)S(1)} %get-tuple-element.10), channel_id=1, source_target_pairs={{64,0},{65,1},{66,2},{67,3},{68,4},{69,5},{70,6},{71,7},{72,8},{73... | collective-permute-start | bytes 393224 | tf_op jit(solution)/shard_map/ppermute | solution.py:104
  222.5 8.9 %copy-start.5 = (bf16[2048,128]{0,1:T(8,128)(2,1)S(1)}, bf16[2048,128]{0,1:T(8,128)(2,1)}, u32[]{:S(2)}) copy-start(bf16[2048,128]{0,1:T(8,128)(2,1)} %copy.13) | copy-start | bytes 1572868
  227.6 3.8 %collective-permute-start.5 = (bf16[2048,128]{0,1:T(8,128)(2,1)S(1)}, bf16[2048,128]{0,1:T(8,128)(2,1)S(1)}, u32[]{:S(2)}, u32[]{:S(2)}) collective-permute-start(bf16[2048,128]{0,1:T(8,128)(2,1)S(1)} %fusion.8), channel_id=1, source_target_pairs={{128,0},{129,1},{130,2},{131,3},{132,4},{133,5},{134,6},{135,7},{1... | collective-permute-start | bytes 1572872 | tf_op jit(solution)/shard_map/ppermute | solution.py:167
  245.4 8.3 %collective-permute-start.6 = (bf16[512,128]{0,1:T(8,128)(2,1)S(1)}, bf16[512,128]{0,1:T(8,128)(2,1)S(1)}, u32[]{:S(2)}, u32[]{:S(2)}) collective-permute-start(bf16[512,128]{0,1:T(8,128)(2,1)S(1)} %get-tuple-element.5), channel_id=1, source_target_pairs={{0,64},{1,65},{2,66},{3,67},{4,68},{5,69},{6,70},{7,71},{8,72},{9,... | collective-permute-start | bytes 393224 | tf_op jit(solution)/shard_map/ppermute | solution.py:104
  246.7 9.8 %collective-permute-start.7 = (bf16[512,128]{0,1:T(8,128)(2,1)S(1)}, bf16[512,128]{0,1:T(8,128)(2,1)S(1)}, u32[]{:S(2)}, u32[]{:S(2)}) collective-permute-start(bf16[512,128]{0,1:T(8,128)(2,1)S(1)} %get-tuple-element.8), channel_id=1, source_target_pairs={{0,64},{1,65},{2,66},{3,67},{4,68},{5,69},{6,70},{7,71},{8,72},{9,... | collective-permute-start | bytes 393224 | tf_op jit(solution)/shard_map/ppermute | solution.py:104
  248.0 11.3 %collective-permute-start.8 = (bf16[512,128]{0,1:T(8,128)(2,1)S(1)}, bf16[512,128]{0,1:T(8,128)(2,1)S(1)}, u32[]{:S(2)}, u32[]{:S(2)}) collective-permute-start(bf16[512,128]{0,1:T(8,128)(2,1)S(1)} %get-tuple-element.7), channel_id=1, source_target_pairs={{0,64},{1,65},{2,66},{3,67},{4,68},{5,69},{6,70},{7,71},{8,72},{9,... | collective-permute-start | bytes 393224 | tf_op jit(solution)/shard_map/ppermute | solution.py:104
  249.3 12.1 %collective-permute-start.9 = (bf16[512,128]{0,1:T(8,128)(2,1)S(1)}, bf16[512,128]{0,1:T(8,128)(2,1)S(1)}, u32[]{:S(2)}, u32[]{:S(2)}) collective-permute-start(bf16[512,128]{0,1:T(8,128)(2,1)S(1)} %get-tuple-element.6), channel_id=1, source_target_pairs={{0,64},{1,65},{2,66},{3,67},{4,68},{5,69},{6,70},{7,71},{8,72},{9,... | collective-permute-start | bytes 393224 | tf_op jit(solution)/shard_map/ppermute | solution.py:104
Sparse Core Ops, SparseCore 0:
  16.8 30.2 all-gather.2
  48.8 114.2 all-gather.4
